TPU v7x, 128 devices: a whole 4x4x4 slice. The times are simulated.
128 devices in a mesh: seq: 16 (over z, x_lo, core), chan: 4 (over y), rep: 2 (over x_hi).
Axes of the slice: x: 4 (x_hi: 2, x_lo: 2; x = x_hi * 2 + x_lo), y: 4, z: 4, core: 2. Of those that a mesh axis runs over, the one named last changes fastest.
Arguments:
- inputs: bfloat16 [2, 4096, 2048], P('rep', 'seq', 'chan'), may hold values from -6 to 6
- w_in: bfloat16 [2048, 1536], P('chan'), may hold values from -0.25 to 0.25
- w_out: bfloat16 [2048, 2048], P('chan'), may hold values from -0.125 to 0.125
- filt_fwd: float32 [4096, 2048], P('seq', 'chan'), may hold values from -0.09375 to 0.09375
- filt_bwd: float32 [4096, 2048], P('seq', 'chan'), may hold values from -0.09375 to 0.09375
- skip_gain: float32 [2048], P('chan'), may hold values from -4 to 4
- cotangent: bfloat16 [2, 4096, 2048], P('rep', 'seq', 'chan'), may hold values from -6 to 6
Outputs:
- layer_out: bfloat16 [2, 4096, 2048], P('rep', 'seq', 'chan')
- d_input: bfloat16 [2, 4096, 2048], P('rep', 'seq', 'chan')
- d_w_in: float32 [2048, 1536], P('chan')
- d_w_out: float32 [2048, 2048], P('chan')
- d_filt_fwd: float32 [4096, 2048], P('seq', 'chan')
- d_filt_bwd: float32 [4096, 2048], P('seq', 'chan')
- d_skip: float32 [2048], P('chan')
All inputs are finite; a program needn't handle non-finite values.
Results may differ from a plain program's by a relative error of at most 0.005.
Values may be sent and summed in bfloat16 or wider, within the bound.
No kernel may reach another device: no remote copies, remote signals or barrier semaphores. Data moves between devices by JAX's collectives and lax.ppermute only.
A program may use at most 128 MiB of HBM per device.

v0:
```python
import math

import jax
import jax.numpy as jnp
import numpy as np
from jax import lax
from jax.sharding import PartitionSpec as P

BLOCK = 512

TABLE_PRECISION = lax.Precision.HIGH


def factor_split(length):
    second = 256
    return length // second, second


def unit_table(size):
    index_row = np.arange(size)
    angle = 2.0 * np.pi * ((index_row[:, None] * index_row[None, :]) % size) / size
    return (jnp.asarray(np.cos(angle), jnp.float32), jnp.asarray(np.sin(angle), jnp.float32))


def twiddle_table(rows, cols):
    length = rows * cols
    phase = (np.arange(rows)[:, None] * np.arange(cols)[None, :]) % length
    angle = 2.0 * np.pi * phase / length
    return (jnp.asarray(np.cos(angle), jnp.float32), jnp.asarray(np.sin(angle), jnp.float32))


def lead_apply(table, fields):
    return jnp.einsum("kn,nrm->krm", table, fields, precision=TABLE_PRECISION)


def minor_apply(fields, table):
    return jnp.einsum("krm,mj->krj", fields, table, precision=TABLE_PRECISION)


def real_spectrum(signal):
    first, field_count, width, second = signal.shape
    cos_a, sin_a = unit_table(first)
    cos_b, sin_b = unit_table(second)
    cos_t, sin_t = twiddle_table(first, second)
    grid = signal.reshape(first, field_count * width, second)
    y_re = lead_apply(cos_a, grid)
    y_im = lead_apply(-sin_a, grid)
    cos_t = cos_t[:, None, :]
    sin_t = sin_t[:, None, :]
    z_re = y_re * cos_t + y_im * sin_t
    z_im = y_im * cos_t - y_re * sin_t
    x_re = minor_apply(z_re, cos_b) + minor_apply(z_im, sin_b)
    x_im = minor_apply(z_im, cos_b) + minor_apply(z_re, -sin_b)
    return x_re.reshape(signal.shape), x_im.reshape(signal.shape)


def real_inverse(spec_re, spec_im):
    first, field_count, width, second = spec_re.shape
    length = first * second
    cos_a, sin_a = unit_table(first)
    cos_b, sin_b = unit_table(second)
    cos_t, sin_t = twiddle_table(first, second)
    flat_re = spec_re.reshape(first, field_count * width, second)
    flat_im = spec_im.reshape(first, field_count * width, second)
    a_re = minor_apply(flat_re, cos_b) + minor_apply(flat_im, -sin_b)
    a_im = minor_apply(flat_im, cos_b) + minor_apply(flat_re, sin_b)
    cos_t = cos_t[:, None, :] * (1.0 / length)
    sin_t = sin_t[:, None, :] * (1.0 / length)
    b_re = a_re * cos_t - a_im * sin_t
    b_im = a_re * sin_t + a_im * cos_t
    out = lead_apply(cos_a, b_re) + lead_apply(-sin_a, b_im)
    return out.reshape(spec_re.shape)


def complex_product(left_re, left_im, right_re, right_im):
    return (left_re * right_re - left_im * right_im, left_re * right_im + left_im * right_re)


def to_channels(fields):
    count = lax.axis_size("seq")
    field_count, rows, width = fields.shape
    parts = fields.reshape(field_count, rows, count, width // count).transpose(2, 0, 3, 1)
    return lax.all_to_all(parts, "seq", split_axis=0, concat_axis=0, tiled=True)


def to_rows(fields):
    count, field_count, width, rows = fields.shape
    gathered = lax.all_to_all(fields, "seq", split_axis=0, concat_axis=0, tiled=True)
    return gathered.transpose(1, 3, 0, 2).reshape(field_count, rows, count * width)


def rep_sum(value):
    count = lax.axis_size("rep")
    total = value
    for shift in range(1, count):
        pairs = [(i, (i + shift) % count) for i in range(count)]
        total = total + lax.ppermute(value, "rep", pairs)
    return total


def chan_reduce_scatter(terms):
    count = lax.axis_size("chan")
    rows, total_width = terms.shape
    pieces = terms.reshape(rows, count, total_width // count).transpose(1, 0, 2)
    received = lax.all_to_all(pieces, "chan", split_axis=0, concat_axis=0, tiled=True)
    total = received[0]
    for index in range(1, count):
        total = total + received[index]
    return total


def on_device(inputs, w_in, w_out, filt_fwd, filt_bwd, skip_gain, cotangent):
    input_rows = inputs[0]
    row_count, chan_width = input_rows.shape
    block_count = chan_width // BLOCK
    input_blocks = input_rows.reshape(row_count, block_count, BLOCK)
    w_blocks = w_in.reshape(block_count, BLOCK, 3, BLOCK)
    grad_rows = cotangent[0]
    piece = lax.all_gather(grad_rows, "chan", axis=1, tiled=True)
    projected = jnp.einsum(
        "mni,nisj->smnj", input_blocks, w_blocks, preferred_element_type=jnp.float32
    )
    projected = projected.reshape(3, row_count, chan_width)
    keys, values, queries = (projected[0], projected[1], projected[2])
    mixed = keys * values
    spread = to_channels(jnp.stack([mixed, filt_fwd, filt_bwd]))
    spec_re, spec_im = real_spectrum(spread)
    mix_re, mix_im = (spec_re[:, 0], spec_im[:, 0])
    gain_re = spec_re[:, 1] + spec_re[:, 2]
    gain_im = spec_im[:, 1] - spec_im[:, 2]
    grad_gated = lax.dot_general(
        piece, w_out, (((1,), (1,)), ((), ())), preferred_element_type=jnp.float32
    )
    grad_conv = grad_gated * queries
    grad_cs = to_channels(grad_conv[None])
    grad_re, grad_im = real_spectrum(grad_cs)
    grad_re, grad_im = (grad_re[:, 0], grad_im[:, 0])
    joint_re, joint_im = complex_product(gain_re, gain_im, mix_re, mix_im)
    back_re, back_im = complex_product(gain_re, -gain_im, grad_re, grad_im)
    both = to_rows(
        real_inverse(
            jnp.stack([joint_re, back_re], axis=1), jnp.stack([joint_im, back_im], axis=1)
        )
    )
    long_conv = both[0]
    back = both[1]
    cross_re, cross_im = complex_product(grad_re, grad_im, mix_re, -mix_im)
    cross = real_inverse(
        jnp.stack([cross_re, cross_re], axis=1), jnp.stack([cross_im, -cross_im], axis=1)
    )
    scale = 1.0 / math.sqrt(lax.axis_size("rep") * lax.axis_size("seq") * row_count)
    skip_part = jnp.sum(grad_cs * spread[:, :1], axis=(0, 3))
    skip_field = jnp.broadcast_to(skip_part[None, :, :, None], grad_cs.shape)
    filt_grads = to_rows(rep_sum(jnp.concatenate([cross, skip_field], axis=1) * scale))
    conv_out = long_conv + skip_gain * mixed
    gated = (queries * conv_out).astype(jnp.bfloat16)
    out_terms = jnp.dot(gated, w_out, preferred_element_type=jnp.float32)
    layer_out = chan_reduce_scatter(out_terms).astype(jnp.bfloat16)
    grad_wout = lax.dot_general(
        gated, piece, (((0,), (0,)), ((), ())), preferred_element_type=jnp.float32
    )
    grad_queries = grad_gated * conv_out
    grad_mixed = back + skip_gain * grad_conv
    grad_pre = jnp.stack([grad_mixed * values, grad_mixed * keys, grad_queries]).astype(
        jnp.bfloat16
    )
    pre_blocks = grad_pre.reshape(3, row_count, block_count, BLOCK)
    d_input = jnp.einsum("smnj,nisj->mni", pre_blocks, w_blocks, preferred_element_type=jnp.float32)
    d_input = d_input.reshape(row_count, chan_width).astype(jnp.bfloat16)
    grad_win = jnp.einsum(
        "mni,smnj->nisj", input_blocks, pre_blocks, preferred_element_type=jnp.float32
    )
    grad_win = grad_win.reshape(chan_width, 3 * BLOCK) * scale
    grad_win, grad_wout = lax.psum((grad_win, grad_wout * scale), ("seq", "rep"))
    return (
        layer_out[None],
        d_input[None],
        grad_win,
        grad_wout,
        filt_grads[0],
        filt_grads[1],
        filt_grads[2, 0],
    )


def solution(mesh):
    return jax.shard_map(
        on_device,
        mesh=mesh,
        in_specs=(
            P("rep", "seq", "chan"),
            P("chan", None),
            P("chan", None),
            P("seq", "chan"),
            P("seq", "chan"),
            P("chan"),
            P("rep", "seq", "chan"),
        ),
        out_specs=(
            P("rep", "seq", "chan"),
            P("rep", "seq", "chan"),
            P("chan", None),
            P("chan", None),
            P("seq", "chan"),
            P("seq", "chan"),
            P("chan"),
        ),
        check_vma=False,
    )
```

profile of v0, /device:TPU:6, one launch (start us, length us, event | category | flops | bytes accessed | tf_op | source)
XLA Modules:
  0.0 281.4 jit_solution(3837587854606809959)
XLA Ops:
  7.2 2.2 copy.162
  9.4 2.0 copy.163
  13.4 1.1 copy-done.14
  14.9 1.3 copy.164
  16.2 6.8 %all-to-all-start = ((f32[16,3,32,256]{3,2,1,0:T(8,128)}), f32[16,3,32,256]{3,2,1,0:T(8,128)S(1)}, u32[]{:S(2)}, u32[]{:S(2)}) async-start(f32[16,3,32,256]{3,2,1,0:T(8,128)} %copy.164), calls=%async_computation | async-start | bytes 3145728 | tf_op jit(solution)/shard_map/all_to_all | solution.py:83
  23.7 20.2 %all-to-all-done = f32[16,3,32,256]{3,2,1,0:T(8,128)S(1)} async-done(((f32[16,3,32,256]{3,2,1,0:T(8,128)}), f32[16,3,32,256]{3,2,1,0:T(8,128)S(1)}, u32[]{:S(2)}, u32[]{:S(2)}) %all-to-all-start) | async-done | bytes 1572896 | tf_op jit(solution)/shard_map/all_to_all | solution.py:83
  43.9 0.9 copy.165
  45.1 0.8 fusion.66
  46.0 1.1 multiply_add_fusion
  47.1 1.6 fusion.5
  48.7 1.6 fusion.1
  50.3 2.7 convolution_add_fusion.1
  53.0 2.7 convolution_add_fusion
  55.7 3.6 %bitcast_multiply_fusion.12 = (f32[256,512]{0,1:T(8,128)}, f32[256,512]{0,1:T(8,128)}) fusion(f32[3,256,1,512]{1,3,2,0:T(8,128)S(1)} %bitcast.259, bf16[512,2048]{1,0:T(8,128)(2,1)} %param.33, bf16[1,256,2048]{2,1,0:T(8,128)(2,1)} %all-gather.3.cloned.1.call-done), kind=kOutput, calls=%fused_computation.88 | convolution fusion | flops 537001984 | bytes 4718592 | tf_op jit(solution)/shard_map/dot_general | solution.py:131
  59.4 4.7 %all-to-all-start.1 = ((f32[16,1,32,256]{3,2,1,0:T(8,128)}), f32[16,1,32,256]{3,2,1,0:T(8,128)S(1)}, u32[]{:S(2)}, u32[]{:S(2)}) async-start(f32[16,1,32,256]{3,2,1,0:T(8,128)} %bitcast.26), calls=%async_computation.1 | async-start | bytes 1048576 | tf_op jit(solution)/shard_map/all_to_all | solution.py:83
  64.1 3.0 %fusion.25 = (f32[16,1,32,256]{3,2,0,1:T(8,128)}, f32[16,1,32,256]{3,2,0,1:T(8,128)S(1)}, f32[16,1,32,256]{3,2,0,1:T(8,128)S(1)}) fusion(f32[16,3,32,256]{3,2,1,0:T(8,128)} %bitcast.269, f32[16,3,32,256]{3,2,1,0:T(8,128)} %bitcast.266), kind=kLoop, calls=%fused_computation.65 | loop fusion | flops 655360 | bytes 4718592 | tf_op jit(solution)/shard_map/sub | solution.py:76
  67.8 2.2 fusion.26
  70.0 3.8 %all-to-all-done.1 = f32[16,1,32,256]{3,2,1,0:T(8,128)S(1)} async-done(((f32[16,1,32,256]{3,2,1,0:T(8,128)}), f32[16,1,32,256]{3,2,1,0:T(8,128)S(1)}, u32[]{:S(2)}, u32[]{:S(2)}) %all-to-all-start.1) | async-done | bytes 524320 | tf_op jit(solution)/shard_map/all_to_all | solution.py:83
  77.0 2.1 negate_bitcast_fusion
  85.1 1.9 multiply_add_fusion.1
  86.9 1.1 fusion.16
  88.0 1.4 convolution_add_fusion.3
  89.4 1.6 copy.187
  91.0 5.3 %all-to-all-start.2 = ((f32[16,2,32,256]{3,2,1,0:T(8,128)}), f32[16,2,32,256]{3,2,1,0:T(8,128)}, u32[]{:S(2)}, u32[]{:S(2)}) async-start(f32[16,2,32,256]{3,2,1,0:T(8,128)} %copy.187), calls=%async_computation.2 | async-start | bytes 2097152 | tf_op jit(solution)/shard_map/all_to_all | solution.py:88
  96.3 3.9 %copy.207 = bf16[2048,512]{1,0:T(8,128)(2,1)} copy(bf16[2048,512]{0,1:T(8,128)(2,1)} %bitcast.280) | data formatting | bytes 4194304 | tf_op jit(solution)/shard_map/dot_general | solution.py:157
  100.3 2.2 fusion.13
  102.5 1.1 convolution_add_fusion.2
  104.2 1.2 fusion.18
  105.6 1.3 maximum_multiply_fusion
  106.9 1.4 collective-permute-start
  108.2 3.5 %all-to-all-done.2 = f32[16,2,32,256]{3,2,1,0:T(8,128)} async-done(((f32[16,2,32,256]{3,2,1,0:T(8,128)}), f32[16,2,32,256]{3,2,1,0:T(8,128)}, u32[]{:S(2)}, u32[]{:S(2)}) %all-to-all-start.2) | async-done | bytes 1048608 | tf_op jit(solution)/shard_map/all_to_all | solution.py:88
  111.8 1.3 fusion.63
  113.1 1.5 fusion.49
  114.8 2.2 fusion
  117.0 2.8 convolution_multiply_fusion.1
  119.8 4.1 %convolution_bitcast_fusion = f32[4,256,512]{2,1,0:T(8,128)} fusion(bf16[4,512,512]{2,1,0:T(8,128)(2,1)} %bitcast.281, f32[1,256,1,512]{1,3,2,0:T(8,128)} %bitcast.287, f32[1,256,1,512]{1,3,2,0:T(8,128)} %copy-done.7, f32[3,256,1,512]{1,3,2,0:T(8,128)S(1)} %bitcast.263, f32[512]{0:T(512)S(1)} %copy-done.29), kind=kOutput, calls=%fused_computation.3 | convolution fusion | flops 537395200 | bytes 5769216 | tf_op jit(solution)/shard_map/dot_general | solution.py:157
  123.9 4.5 %all-to-all-start.3 = ((f32[4,256,512]{2,1,0:T(8,128)}), f32[4,256,512]{2,1,0:T(8,128)}, u32[]{:S(2)}, u32[]{:S(2)}) async-start(f32[4,256,512]{2,1,0:T(8,128)} %convolution_bitcast_fusion), calls=%async_computation.3 | async-start | bytes 4194304 | tf_op jit(solution)/shard_map/all_to_all | solution.py:105
  128.4 24.7 %collective-permute-done = f32[16,3,32,256]{3,2,1,0:T(8,128)} collective-permute-done((f32[16,3,32,256]{3,2,1,0:T(8,128)}, f32[16,3,32,256]{3,2,1,0:T(8,128)}, u32[]{:S(2)}, u32[]{:S(2)}) %collective-permute-start) | collective-permute-done | bytes 1572896 | tf_op jit(solution)/shard_map/ppermute | solution.py:97
  153.1 2.9 %fusion.57 = f32[16,3,32,256]{3,2,1,0:T(8,128)} fusion(f32[16,3,32,256]{3,2,1,0:T(8,128)} %collective-permute-done, f32[16,1,32,256]{3,2,1,0:T(8,128)S(1)} %broadcast_in_dim.2, f32[16,2,32,256]{3,2,1,0:T(8,128)S(1)} %copy.197), kind=kLoop, calls=%fused_computation.116 | loop fusion | flops 1179648 | bytes 4718592 | tf_op jit(solution)/shard_map/add | solution.py:97
  155.9 5.9 %all-to-all-start.4 = ((f32[16,3,32,256]{3,2,1,0:T(8,128)}), f32[16,3,32,256]{3,2,1,0:T(8,128)S(1)}, u32[]{:S(2)}, u32[]{:S(2)}) async-start(f32[16,3,32,256]{3,2,1,0:T(8,128)} %fusion.57), calls=%async_computation.4 | async-start | bytes 3145728 | tf_op jit(solution)/shard_map/all_to_all | solution.py:88
  161.8 2.5 fusion.8
  164.3 2.4 fusion.19
  166.7 17.3 %all-to-all-done.4 = f32[16,3,32,256]{3,2,1,0:T(8,128)S(1)} async-done(((f32[16,3,32,256]{3,2,1,0:T(8,128)}), f32[16,3,32,256]{3,2,1,0:T(8,128)S(1)}, u32[]{:S(2)}, u32[]{:S(2)}) %all-to-all-start.4) | async-done | bytes 1572896 | tf_op jit(solution)/shard_map/all_to_all | solution.py:88
  184.3 1.0 copy.201
  185.3 1.0 copy.200
  187.0 79.3 %all-reduce.3.cloned.1.call-done = (f32[512,1536]{0,1:T(8,128)}, f32[512,2048]{1,0:T(8,128)}) async-done(((f32[512,1536]{0,1:T(8,128)}, f32[512,2048]{1,0:T(8,128)}), (f32[512,1536]{0,1:T(8,128)}, f32[512,2048]{1,0:T(8,128)})) %all-reduce.3.cloned.1.call-update) | async-done | bytes 7340048 | tf_op jit(solution)/shard_map/psum | solution.py:174
  266.3 3.5 %copy.199 = f32[512,1536]{1,0:T(8,128)} copy(f32[512,1536]{0,1:T(8,128)} %get-tuple-element.35) | data formatting | bytes 6291456
  269.9 4.7 %copy.255 = f32[512,2048]{1,0:T(8,128)} copy(f32[512,2048]{1,0:T(8,128)} %get-tuple-element.76) | data formatting | bytes 8388608
  (93 shorter events, 15.0 us)
Async XLA Ops:
  7.2 5.0 %copy-start = (bf16[1,256,512]{2,1,0:T(8,128)(2,1)S(1)}, bf16[1,256,512]{2,1,0:T(8,128)(2,1)}, u32[]{:S(2)}) copy-start(bf16[1,256,512]{2,1,0:T(8,128)(2,1)} %param.31) | copy-start | bytes 786436
  7.2 4.2 %copy-start.19 = (bf16[512,1536]{1,0:T(8,128)(2,1)S(1)}, bf16[512,1536]{1,0:T(8,128)(2,1)}, u32[]{:S(2)}) copy-start(bf16[512,1536]{1,0:T(8,128)(2,1)} %param.32) | copy-start | bytes 4718596
  12.1 1.2 copy-start.3
  13.3 1.2 copy-start.14
  13.3 1.4 copy-start.15
  13.4 1.5 copy-start.7
  16.2 27.8 %all-to-all-start = ((f32[16,3,32,256]{3,2,1,0:T(8,128)}), f32[16,3,32,256]{3,2,1,0:T(8,128)S(1)}, u32[]{:S(2)}, u32[]{:S(2)}) async-start(f32[16,3,32,256]{3,2,1,0:T(8,128)} %copy.164), calls=%async_computation | async-start | bytes 3145728 | tf_op jit(solution)/shard_map/all_to_all | solution.py:83
  23.0 32.8 %all-gather.3.cloned.1.call-start = ((), (), s32[]{:S(2)}) async-start(), calls=%async_computation.5 | async-start | bytes 1310720 | tf_op jit(solution)/shard_map/all_gather | solution.py:119
  23.7 21.4 %copy-start.23 = (f32[16,16,1]{1,0,2:T(8,128)S(1)}, f32[16,16,1]{1,0,2:T(8,128)}, u32[]{:S(2)}) copy-start(f32[16,16,1]{1,0,2:T(8,128)} %constant.32) | copy-start | bytes 3076
  43.9 1.2 copy-start.2
  45.1 0.8 copy-start.24
  45.1 0.8 copy-start.25
  45.1 0.8 copy-start.26
  46.0 1.1 copy-start.1
  48.7 1.6 copy-start.9
  50.3 2.7 copy-start.12
  59.4 14.4 %all-to-all-start.1 = ((f32[16,1,32,256]{3,2,1,0:T(8,128)}), f32[16,1,32,256]{3,2,1,0:T(8,128)S(1)}, u32[]{:S(2)}, u32[]{:S(2)}) async-start(f32[16,1,32,256]{3,2,1,0:T(8,128)} %bitcast.26), calls=%async_computation.1 | async-start | bytes 1048576 | tf_op jit(solution)/shard_map/all_to_all | solution.py:83
  67.0 0.8 copy-start.5
  75.1 1.3 copy-start.13
  75.7 1.3 copy-start.6
  80.7 1.0 copy-start.17
  80.7 1.2 copy-start.18
  84.1 1.0 copy-start.10
  84.1 0.9 copy-start.27
  84.1 0.9 copy-start.28
  91.0 20.8 %all-to-all-start.2 = ((f32[16,2,32,256]{3,2,1,0:T(8,128)}), f32[16,2,32,256]{3,2,1,0:T(8,128)}, u32[]{:S(2)}, u32[]{:S(2)}) async-start(f32[16,2,32,256]{3,2,1,0:T(8,128)} %copy.187), calls=%async_computation.2 | async-start | bytes 2097152 | tf_op jit(solution)/shard_map/all_to_all | solution.py:88
  96.3 170.0 %all-reduce.3.cloned.1.call-start = ((), (), s32[]{:S(2)}) async-start(), calls=%async_computation.6 | async-start | bytes 14680064 | tf_op jit(solution)/shard_map/psum | solution.py:174
  106.8 6.3 %copy-start.29 = (f32[512]{0:T(512)S(1)}, f32[512]{0:T(512)}, u32[]{:S(2)}) copy-start(f32[512]{0:T(512)} %param.36) | copy-start | bytes 6148
  106.9 46.2 %collective-permute-start = (f32[16,3,32,256]{3,2,1,0:T(8,128)}, f32[16,3,32,256]{3,2,1,0:T(8,128)}, u32[]{:S(2)}, u32[]{:S(2)}) collective-permute-start(f32[16,3,32,256]{3,2,1,0:T(8,128)} %maximum_multiply_fusion), channel_id=1, source_target_pairs={{0,1},{1,0},{2,3},{3,2},{4,5},{5,4},{6,7},{7,6},{8,9},{9,8},{10,11... | collective-permute-start | bytes 4718600 | tf_op jit(solution)/shard_map/ppermute | solution.py:97
  111.8 1.4 copy-start.16
  113.1 1.5 copy-start.8
  114.6 2.4 copy-start.20
  114.6 2.4 copy-start.21
  114.6 2.4 copy-start.22
  114.8 2.3 copy-start.11
  123.9 32.0 %all-to-all-start.3 = ((f32[4,256,512]{2,1,0:T(8,128)}), f32[4,256,512]{2,1,0:T(8,128)}, u32[]{:S(2)}, u32[]{:S(2)}) async-start(f32[4,256,512]{2,1,0:T(8,128)} %convolution_bitcast_fusion), calls=%async_computation.3 | async-start | bytes 4194304 | tf_op jit(solution)/shard_map/all_to_all | solution.py:105
  155.9 5.9 %copy-start.4 = (bf16[512,1536]{0,1:T(8,128)(2,1)S(1)}, bf16[512,1536]{0,1:T(8,128)(2,1)}, u32[]{:S(2)}) copy-start(bf16[512,1536]{0,1:T(8,128)(2,1)} %copy-done.3) | copy-start | bytes 4718596
  155.9 28.1 %all-to-all-start.4 = ((f32[16,3,32,256]{3,2,1,0:T(8,128)}), f32[16,3,32,256]{3,2,1,0:T(8,128)S(1)}, u32[]{:S(2)}, u32[]{:S(2)}) async-start(f32[16,3,32,256]{3,2,1,0:T(8,128)} %fusion.57), calls=%async_computation.4 | async-start | bytes 3145728 | tf_op jit(solution)/shard_map/all_to_all | solution.py:88
Sparse Core Ops, SparseCore 0:
  25.4 25.0 all-gather.2
  119.9 146.3 all-reduce.2
where the time goes:
time: 282 us; the launch traced here: 281 us
  waiting for transfers between devices  150 us (53%)
  matrix products  43.3 us (15%)
  local copies, waits for them, and re-layouts  30.2 us (11%)
  starting transfers between devices  28.6 us (10%)
  other arithmetic  15.2 us (5%)
  between operations  14.6 us (5%)
    psum x1, waiting for transfers between devices, on_device(): lax.psum((grad_win, grad_wout * scale), ('seq', 'rep'))  79.3 us
    ppermute x1, waiting for transfers between devices, rep_sum(): total = total + lax.ppermute(value, 'rep', pairs)  24.7 us
    all_to_all x2, waiting for transfers between devices, to_channels(): return lax.all_to_all(parts, 'seq', split_axis=0, concat_axis=0, tiled=True)  24 us
    all_to_all x2, waiting for transfers between devices, to_rows(): lax.all_to_all(fields, 'seq', split_axis=0, concat_axis=0, tiled=True)  20.9 us
    unnamed x67, local copies, waits for them, and re-layouts  19.1 us
    dot_general x16, matrix products, minor_apply(): return jnp.einsum('krm,mj->krj', fields, table, precision=TABLE_PRECISION)  18.5 us
    all_to_all x2, starting transfers between devices, to_channels(): return lax.all_to_all(parts, 'seq', split_axis=0, concat_axis=0, tiled=True)  11.5 us
    all_to_all x2, starting transfers between devices, to_rows(): lax.all_to_all(fields, 'seq', split_axis=0, concat_axis=0, tiled=True)  11.2 us
  transfers between devices with their start and end apart: 8, of which 6 were waited for; matrix products, arithmetic and copies ran while one was open for 18% of the time, Pallas kernels for 0%

commit v1 on v0

--- a/solution.py
+++ b/solution.py
@@ -116,25 +116,27 @@
     input_blocks = input_rows.reshape(row_count, block_count, BLOCK)
     w_blocks = w_in.reshape(block_count, BLOCK, 3, BLOCK)
     grad_rows = cotangent[0]
-    piece = lax.all_gather(grad_rows, "chan", axis=1, tiled=True)
+    chan_count = lax.axis_size("chan")
+    copies = jnp.broadcast_to(grad_rows[None], (chan_count,) + grad_rows.shape)
+    gathered = lax.all_to_all(copies, "chan", split_axis=0, concat_axis=0, tiled=True)
+    piece = gathered.transpose(1, 0, 2).reshape(grad_rows.shape[0], -1)
     projected = jnp.einsum(
         "mni,nisj->smnj", input_blocks, w_blocks, preferred_element_type=jnp.float32
     )
     projected = projected.reshape(3, row_count, chan_width)
     keys, values, queries = (projected[0], projected[1], projected[2])
     mixed = keys * values
-    spread = to_channels(jnp.stack([mixed, filt_fwd, filt_bwd]))
+    grad_gated = lax.dot_general(
+        piece, w_out, (((1,), (1,)), ((), ())), preferred_element_type=jnp.float32
+    )
+    grad_conv = grad_gated * queries
+    spread = to_channels(jnp.stack([mixed, filt_fwd, filt_bwd, grad_conv]))
     spec_re, spec_im = real_spectrum(spread)
     mix_re, mix_im = (spec_re[:, 0], spec_im[:, 0])
     gain_re = spec_re[:, 1] + spec_re[:, 2]
     gain_im = spec_im[:, 1] - spec_im[:, 2]
-    grad_gated = lax.dot_general(
-        piece, w_out, (((1,), (1,)), ((), ())), preferred_element_type=jnp.float32
-    )
-    grad_conv = grad_gated * queries
-    grad_cs = to_channels(grad_conv[None])
-    grad_re, grad_im = real_spectrum(grad_cs)
-    grad_re, grad_im = (grad_re[:, 0], grad_im[:, 0])
+    grad_re, grad_im = (spec_re[:, 3], spec_im[:, 3])
+    grad_cs = spread[:, 3:]
     joint_re, joint_im = complex_product(gain_re, gain_im, mix_re, mix_im)
     back_re, back_im = complex_product(gain_re, -gain_im, grad_re, grad_im)
     both = to_rows(

time: 282 us -> 278 us (0.986)
  blocking collectives: 0 us -> 33.1 us
  waiting for transfers between devices: 150 us -> 127 us
  starting transfers between devices: 28.6 us -> 21.9 us
  matrix products: 43.3 us -> 38 us
  other arithmetic: 15.2 us -> 10.1 us
    all_to_all x0 -> x1, blocking collectives: none -> 33.1 us  [to_channels(): return lax.all_to_all(parts, 'seq', split_axis=0, concat_axis=0, tiled=True)]
    all_to_all x2 -> x1, waiting for transfers between devices: 24 us -> 7.52 us  [on_device(): lax.all_to_all(copies, 'chan', split_axis=0, concat_axis=0, tiled=True)]
    all_to_all x2 -> x1, starting transfers between devices: 11.5 us -> 4.59 us  [on_device(): lax.all_to_all(copies, 'chan', split_axis=0, concat_axis=0, tiled=True)]
    psum x1, waiting for transfers between devices: 79.3 us -> 72.5 us  [on_device(): lax.psum((grad_win, grad_wout * scale), ('seq', 'rep'))]
    dot_general x16 -> x12, matrix products: 18.5 us -> 14.9 us  [minor_apply(): return jnp.einsum('krm,mj->krj', fields, table, precision=TABLE_PRECISION)]
    ppermute x1, waiting for transfers between devices: 24.7 us -> 27.7 us  [rep_sum(): total = total + lax.ppermute(value, 'rep', pairs)]
    dot_general x8 -> x6, matrix products: 8.92 us -> 8.05 us  [lead_apply(): return jnp.einsum('kn,nrm->krm', table, fields, precision=TABLE_PRECISION)]
    unnamed x67 -> x77, local copies, waits for them, and re-layouts: 19.1 us -> 18.8 us
  transfers between devices with their start and end apart: 8 -> 6, of which waited for: 6 -> 5; matrix products, arithmetic and copies ran while one was open for 18% -> 14% of each run, Pallas kernels for 0% -> 0%
where the time goes in v1:
time: 278 us; the launch traced here: 277 us
  waiting for transfers between devices  127 us (46%)
  matrix products  38 us (14%)
  blocking collectives  33.1 us (12%)
  local copies, waits for them, and re-layouts  32.3 us (12%)
  starting transfers between devices  21.9 us (8%)
  between operations  14.6 us (5%)
  other arithmetic  10.1 us (4%)
    psum x1, waiting for transfers between devices, on_device(): lax.psum((grad_win, grad_wout * scale), ('seq', 'rep'))  72.5 us
    all_to_all x1, blocking collectives, to_channels(): return lax.all_to_all(parts, 'seq', split_axis=0, concat_axis=0, tiled=True)  33.1 us
    ppermute x1, waiting for transfers between devices, rep_sum(): total = total + lax.ppermute(value, 'rep', pairs)  27.7 us
    all_to_all x2, waiting for transfers between devices, to_rows(): lax.all_to_all(fields, 'seq', split_axis=0, concat_axis=0, tiled=True)  19.1 us
    unnamed x77, local copies, waits for them, and re-layouts  18.8 us
    dot_general x12, matrix products, minor_apply(): return jnp.einsum('krm,mj->krj', fields, table, precision=TABLE_PRECISION)  14.9 us
    all_to_all x2, starting transfers between devices, to_rows(): lax.all_to_all(fields, 'seq', split_axis=0, concat_axis=0, tiled=True)  11.1 us
    dot_general x6, matrix products, lead_apply(): return jnp.einsum('kn,nrm->krm', table, fields, precision=TABLE_PRECISION)  8.05 us
  transfers between devices with their start and end apart: 6, of which 5 were waited for; matrix products, arithmetic and copies ran while one was open for 14% of the time, Pallas kernels for 0%

profile of v1, /device:TPU:6, one launch (start us, length us, event | category | flops | bytes accessed | tf_op | source)
XLA Modules:
  0.0 276.9 jit_solution(15324773571597005903)
XLA Ops:
  7.2 1.2 copy.117
  8.4 1.0 broadcast_in_dim.7
  9.4 4.6 %all-to-all-start = ((bf16[4,256,512]{1,2,0:T(8,128)(2,1)}), bf16[4,256,512]{1,2,0:T(8,128)(2,1)S(1)}, u32[]{:S(2)}, u32[]{:S(2)}) async-start(bf16[4,256,512]{1,2,0:T(8,128)(2,1)} %broadcast_in_dim.7), calls=%async_computation | async-start | bytes 2097152 | tf_op jit(solution)/shard_map/all_to_all | solution.py:121
  14.0 1.0 copy.115
  15.0 2.0 copy.116
  17.0 1.6 copy.111
  18.7 2.0 fusion.34
  20.7 0.9 bitcast_multiply_fusion.4
  21.6 7.5 %all-to-all-done = bf16[4,256,512]{1,2,0:T(8,128)(2,1)S(1)} async-done(((bf16[4,256,512]{1,2,0:T(8,128)(2,1)}), bf16[4,256,512]{1,2,0:T(8,128)(2,1)S(1)}, u32[]{:S(2)}, u32[]{:S(2)}) %all-to-all-start) | async-done | bytes 1048608 | tf_op jit(solution)/shard_map/all_to_all | solution.py:121
  29.1 3.2 %bitcast_multiply_fusion.3 = (f32[256,512]{0,1:T(8,128)S(1)}, f32[256,512]{0,1:T(8,128)}) fusion(f32[3,256,1,512]{1,3,2,0:T(8,128)S(1)} %bitcast.157, bf16[512,2048]{1,0:T(8,128)(2,1)} %param.27, bf16[256,2048]{0,1:T(8,128)(2,1)S(1)} %bitcast.170), kind=kOutput, calls=%fused_computation.60 | convolution fusion | flops 537001984 | bytes 4718592 | tf_op jit(solution)/shard_map/dot_general | solution.py:129
  32.8 33.1 %all_to_all.25 = f32[16,4,32,256]{3,2,1,0:T(8,128)S(1)} all-to-all(f32[16,4,32,256]{3,2,1,0:T(8,128)S(1)} %copy.119), channel_id=1, replica_groups=mesh['seq'=16,'chan'=4,'rep'=2] {'seq'}, dimensions={0} | all-to-all | bytes 4194304 | tf_op jit(solution)/shard_map/all_to_all | solution.py:83
  65.9 1.2 copy.120
  67.2 1.0 fusion.42
  68.3 1.4 multiply_add_fusion
  69.8 2.1 fusion.1
  71.9 2.1 fusion.3
  73.9 2.1 fusion.9
  76.0 2.3 fusion.12
  84.3 2.3 multiply_add_fusion.1
  86.6 1.1 fusion.21
  87.6 1.1 convolution_add_fusion.1
  88.8 1.6 copy.127
  90.4 5.3 %all-to-all-start.2 = ((f32[16,2,32,256]{3,2,1,0:T(8,128)}), f32[16,2,32,256]{3,2,1,0:T(8,128)}, u32[]{:S(2)}, u32[]{:S(2)}) async-start(f32[16,2,32,256]{3,2,1,0:T(8,128)} %copy.127), calls=%async_computation.2 | async-start | bytes 2097152 | tf_op jit(solution)/shard_map/all_to_all | solution.py:88
  95.7 4.2 %copy.145 = bf16[2048,512]{1,0:T(8,128)(2,1)} copy(bf16[2048,512]{0,1:T(8,128)(2,1)} %bitcast.165) | data formatting | bytes 4194304 | tf_op jit(solution)/shard_map/dot_general | solution.py:159
  99.9 2.3 fusion.18
  102.3 1.1 convolution_add_fusion
  105.1 1.3 maximum_multiply_fusion
  106.4 1.4 collective-permute-start
  107.8 3.3 %all-to-all-done.2 = f32[16,2,32,256]{3,2,1,0:T(8,128)} async-done(((f32[16,2,32,256]{3,2,1,0:T(8,128)}), f32[16,2,32,256]{3,2,1,0:T(8,128)}, u32[]{:S(2)}, u32[]{:S(2)}) %all-to-all-start.2) | async-done | bytes 1048608 | tf_op jit(solution)/shard_map/all_to_all | solution.py:88
  111.2 1.4 fusion.41
  113.1 2.2 fusion
  115.4 2.8 convolution_multiply_fusion.1
  118.2 1.6 copy-done.6
  119.7 2.1 convolution_bitcast_fusion
  121.8 4.8 %all-to-all-start.3 = ((f32[4,256,512]{2,1,0:T(8,128)}), f32[4,256,512]{2,1,0:T(8,128)}, u32[]{:S(2)}, u32[]{:S(2)}) async-start(f32[4,256,512]{2,1,0:T(8,128)} %convolution_bitcast_fusion), calls=%async_computation.3 | async-start | bytes 4194304 | tf_op jit(solution)/shard_map/all_to_all | solution.py:105
  126.6 27.7 %collective-permute-done = f32[16,3,32,256]{3,2,1,0:T(8,128)} collective-permute-done((f32[16,3,32,256]{3,2,1,0:T(8,128)}, f32[16,3,32,256]{3,2,1,0:T(8,128)}, u32[]{:S(2)}, u32[]{:S(2)}) %collective-permute-start) | collective-permute-done | bytes 1572896 | tf_op jit(solution)/shard_map/ppermute | solution.py:97
  154.3 3.0 %fusion.37 = f32[16,3,32,256]{3,2,1,0:T(8,128)} fusion(f32[16,3,32,256]{3,2,1,0:T(8,128)} %collective-permute-done, f32[16,1,32,256]{3,2,1,0:T(8,128)S(1)} %copy-done.9, f32[16,2,32,256]{3,2,1,0:T(8,128)S(1)} %copy-done.5), kind=kLoop, calls=%fused_computation.78 | loop fusion | flops 1179648 | bytes 4718592 | tf_op jit(solution)/shard_map/add | solution.py:97
  157.3 5.8 %all-to-all-start.4 = ((f32[16,3,32,256]{3,2,1,0:T(8,128)}), f32[16,3,32,256]{3,2,1,0:T(8,128)S(1)}, u32[]{:S(2)}, u32[]{:S(2)}) async-start(f32[16,3,32,256]{3,2,1,0:T(8,128)} %fusion.37), calls=%async_computation.4 | async-start | bytes 3145728 | tf_op jit(solution)/shard_map/all_to_all | solution.py:88
  163.2 2.8 %fusion.16 = bf16[1,256,512]{2,1,0:T(8,128)(2,1)} fusion(bf16[512,3,512]{0,2,1:T(8,128)(2,1)} %bitcast.179, bf16[1,256,512]{1,2,0:T(8,128)(2,1)S(1)} %bitcast.192, bf16[1,256,512]{1,2,0:T(8,128)(2,1)S(1)} %copy-done.26, bf16[1,256,512]{1,2,0:T(8,128)(2,1)S(1)} %copy-done.22), kind=kOutput, calls=%fused_computation.26 | convolution fusion | flops 403570688 | bytes 2621440 | tf_op jit(solution)/shard_map/smnj,nisj->mni/dot_general | solution.py:170
  165.9 2.4 fusion.24
  168.3 15.8 %all-to-all-done.4 = f32[16,3,32,256]{3,2,1,0:T(8,128)S(1)} async-done(((f32[16,3,32,256]{3,2,1,0:T(8,128)}), f32[16,3,32,256]{3,2,1,0:T(8,128)S(1)}, u32[]{:S(2)}, u32[]{:S(2)}) %all-to-all-start.4) | async-done | bytes 1572896 | tf_op jit(solution)/shard_map/all_to_all | solution.py:88
  184.3 1.2 copy-done.7
  185.6 1.0 copy.139
  186.6 1.0 copy.138
  187.5 1.7 slice_reduce_fusion
  189.3 72.5 %all-reduce.3.cloned.1.call-done = (f32[512,1536]{0,1:T(8,128)}, f32[512,2048]{1,0:T(8,128)}) async-done(((f32[512,1536]{0,1:T(8,128)}, f32[512,2048]{1,0:T(8,128)}), (f32[512,1536]{0,1:T(8,128)}, f32[512,2048]{1,0:T(8,128)})) %all-reduce.3.cloned.1.call-update) | async-done | bytes 7340048 | tf_op jit(solution)/shard_map/psum | solution.py:176
  261.8 3.5 %copy.137 = f32[512,1536]{1,0:T(8,128)} copy(f32[512,1536]{0,1:T(8,128)} %get-tuple-element.35) | data formatting | bytes 6291456
  265.3 4.7 %copy.171 = f32[512,2048]{1,0:T(8,128)} copy(f32[512,2048]{1,0:T(8,128)} %get-tuple-element.73) | data formatting | bytes 8388608
  (93 shorter events, 9.0 us)
Async XLA Ops:
  7.2 11.5 %copy-start = (bf16[1,256,512]{2,1,0:T(8,128)(2,1)S(1)}, bf16[1,256,512]{2,1,0:T(8,128)(2,1)}, u32[]{:S(2)}) copy-start(bf16[1,256,512]{2,1,0:T(8,128)(2,1)} %param.25) | copy-start | bytes 786436
  7.2 6.8 %copy-start.27 = (f32[256,512]{1,0:T(8,128)S(1)}, f32[256,512]{1,0:T(8,128)}, u32[]{:S(2)}) copy-start(f32[256,512]{1,0:T(8,128)} %param.28) | copy-start | bytes 1572868
  9.4 7.6 %copy-start.20 = (bf16[512,1536]{1,0:T(8,128)(2,1)S(1)}, bf16[512,1536]{1,0:T(8,128)(2,1)}, u32[]{:S(2)}) copy-start(bf16[512,1536]{1,0:T(8,128)(2,1)} %param.26) | copy-start | bytes 4718596
  9.4 19.7 %all-to-all-start = ((bf16[4,256,512]{1,2,0:T(8,128)(2,1)}), bf16[4,256,512]{1,2,0:T(8,128)(2,1)S(1)}, u32[]{:S(2)}, u32[]{:S(2)}) async-start(bf16[4,256,512]{1,2,0:T(8,128)(2,1)} %broadcast_in_dim.7), calls=%async_computation | async-start | bytes 2097152 | tf_op jit(solution)/shard_map/all_to_all | solution.py:121
  29.1 3.2 %copy-start.10 = (f32[1,256,1,512]{1,3,2,0:T(8,128)S(1)}, f32[1,256,1,512]{1,3,2,0:T(8,128)}, u32[]{:S(2)}) copy-start(f32[1,256,1,512]{1,3,2,0:T(8,128)} %bitcast_multiply_fusion.4) | copy-start | bytes 1572868
  29.1 3.2 %copy-start.18 = (f32[256,512]{0,1:T(8,128)S(1)}, f32[256,512]{0,1:T(8,128)}, u32[]{:S(2)}) copy-start(f32[256,512]{0,1:T(8,128)} %copy.115) | copy-start | bytes 1572868
  29.1 3.2 %copy-start.19 = (f32[256,512]{0,1:T(8,128)S(1)}, f32[256,512]{0,1:T(8,128)}, u32[]{:S(2)}) copy-start(f32[256,512]{0,1:T(8,128)} %copy.116) | copy-start | bytes 1572868
  65.9 1.3 copy-start.1
  65.9 1.3 copy-start.28
  67.2 1.0 copy-start.29
  67.2 1.0 copy-start.32
  67.2 1.1 copy-start.33
  68.3 1.5 copy-start.3
  69.8 2.1 copy-start.14
  73.9 2.1 copy-start.15
  83.6 0.7 copy-start.30
  83.6 0.7 copy-start.31
  90.4 20.8 %all-to-all-start.2 = ((f32[16,2,32,256]{3,2,1,0:T(8,128)}), f32[16,2,32,256]{3,2,1,0:T(8,128)}, u32[]{:S(2)}, u32[]{:S(2)}) async-start(f32[16,2,32,256]{3,2,1,0:T(8,128)} %copy.127), calls=%async_computation.2 | async-start | bytes 2097152 | tf_op jit(solution)/shard_map/all_to_all | solution.py:88
  95.7 166.1 %all-reduce.3.cloned.1.call-start = ((), (), s32[]{:S(2)}) async-start(), calls=%async_computation.5 | async-start | bytes 14680064 | tf_op jit(solution)/shard_map/psum | solution.py:176
  99.9 2.3 copy-start.12
  102.3 1.7 copy-start.2
  104.0 2.4 copy-start.4
  104.3 0.8 copy-start.8
  105.1 7.4 %copy-start.34 = (f32[512]{0:T(512)S(1)}, f32[512]{0:T(512)}, u32[]{:S(2)}) copy-start(f32[512]{0:T(512)} %param.30) | copy-start | bytes 6148
  106.4 47.8 %collective-permute-start = (f32[16,3,32,256]{3,2,1,0:T(8,128)}, f32[16,3,32,256]{3,2,1,0:T(8,128)}, u32[]{:S(2)}, u32[]{:S(2)}) collective-permute-start(f32[16,3,32,256]{3,2,1,0:T(8,128)} %maximum_multiply_fusion), channel_id=1, source_target_pairs={{0,1},{1,0},{2,3},{3,2},{4,5},{5,4},{6,7},{7,6},{8,9},{9,8},{10,11... | collective-permute-start | bytes 4718600 | tf_op jit(solution)/shard_map/ppermute | solution.py:97
  111.2 1.4 copy-start.11
  111.2 1.6 copy-start.13
  112.7 2.7 copy-start.16
  113.0 2.4 copy-start.21
  113.0 2.4 copy-start.23
  113.0 2.4 copy-start.25
  118.2 1.6 copy-start.6
  118.2 1.6 copy-start.17
  121.8 32.5 %copy-start.5 = (f32[16,2,32,256]{3,2,1,0:T(8,128)S(1)}, f32[16,2,32,256]{3,2,1,0:T(8,128)}, u32[]{:S(2)}) copy-start(f32[16,2,32,256]{3,2,1,0:T(8,128)} %copy-done.4) | copy-start | bytes 3145732
  121.8 32.5 %copy-start.9 = (f32[16,1,32,256]{3,2,1,0:T(8,128)S(1)}, f32[16,1,32,256]{3,2,1,0:T(8,128)}, u32[]{:S(2)}) copy-start(f32[16,1,32,256]{3,2,1,0:T(8,128)} %copy-done.8) | copy-start | bytes 1572868
  121.8 35.5 %all-to-all-start.3 = ((f32[4,256,512]{2,1,0:T(8,128)}), f32[4,256,512]{2,1,0:T(8,128)}, u32[]{:S(2)}, u32[]{:S(2)}) async-start(f32[4,256,512]{2,1,0:T(8,128)} %convolution_bitcast_fusion), calls=%async_computation.3 | async-start | bytes 4194304 | tf_op jit(solution)/shard_map/all_to_all | solution.py:105
  157.3 5.8 %copy-start.22 = (bf16[1,256,512]{1,2,0:T(8,128)(2,1)S(1)}, bf16[1,256,512]{1,2,0:T(8,128)(2,1)}, u32[]{:S(2)}) copy-start(bf16[1,256,512]{1,2,0:T(8,128)(2,1)} %copy-done.21) | copy-start | bytes 786436
  157.3 5.8 %copy-start.24 = (bf16[256,512]{0,1:T(8,128)(2,1)S(1)}, bf16[256,512]{0,1:T(8,128)(2,1)}, u32[]{:S(2)}) copy-start(bf16[256,512]{0,1:T(8,128)(2,1)} %copy-done.23) | copy-start | bytes 786436
  157.3 5.9 %copy-start.26 = (bf16[1,256,512]{1,2,0:T(8,128)(2,1)S(1)}, bf16[1,256,512]{1,2,0:T(8,128)(2,1)}, u32[]{:S(2)}) copy-start(bf16[1,256,512]{1,2,0:T(8,128)(2,1)} %copy-done.25) | copy-start | bytes 786436
  157.3 26.8 %all-to-all-start.4 = ((f32[16,3,32,256]{3,2,1,0:T(8,128)}), f32[16,3,32,256]{3,2,1,0:T(8,128)S(1)}, u32[]{:S(2)}, u32[]{:S(2)}) async-start(f32[16,3,32,256]{3,2,1,0:T(8,128)} %fusion.37), calls=%async_computation.4 | async-start | bytes 3145728 | tf_op jit(solution)/shard_map/all_to_all | solution.py:88
  184.2 1.2 copy-start.7
Sparse Core Ops, SparseCore 0:
  118.3 143.4 all-reduce.2

commit v2 on v1

--- a/solution.py
+++ b/solution.py
@@ -130,13 +130,14 @@
         piece, w_out, (((1,), (1,)), ((), ())), preferred_element_type=jnp.float32
     )
     grad_conv = grad_gated * queries
-    spread = to_channels(jnp.stack([mixed, filt_fwd, filt_bwd, grad_conv]))
+    filt_re, filt_im = real_spectrum(to_channels(jnp.stack([filt_fwd, filt_bwd])))
+    gain_re = filt_re[:, 0] + filt_re[:, 1]
+    gain_im = filt_im[:, 0] - filt_im[:, 1]
+    spread = to_channels(jnp.stack([mixed, grad_conv]))
     spec_re, spec_im = real_spectrum(spread)
     mix_re, mix_im = (spec_re[:, 0], spec_im[:, 0])
-    gain_re = spec_re[:, 1] + spec_re[:, 2]
-    gain_im = spec_im[:, 1] - spec_im[:, 2]
-    grad_re, grad_im = (spec_re[:, 3], spec_im[:, 3])
-    grad_cs = spread[:, 3:]
+    grad_re, grad_im = (spec_re[:, 1], spec_im[:, 1])
+    grad_cs = spread[:, 1:]
     joint_re, joint_im = complex_product(gain_re, gain_im, mix_re, mix_im)
     back_re, back_im = complex_product(gain_re, -gain_im, grad_re, grad_im)
     both = to_rows(

time: 278 us -> 286 us (1.029)
  blocking collectives: 33.1 us -> 0 us
  waiting for transfers between devices: 127 us -> 152 us
  starting transfers between devices: 21.9 us -> 34.1 us
    all_to_all x1 -> x0, blocking collectives: 33.1 us -> none  [to_channels(): return lax.all_to_all(parts, 'seq', split_axis=0, concat_axis=0, tiled=True)]
    all_to_all x0 -> x2, waiting for transfers between devices: none -> 22.6 us  [to_channels(): return lax.all_to_all(parts, 'seq', split_axis=0, concat_axis=0, tiled=True)]
    all_to_all x0 -> x2, starting transfers between devices: none -> 12.2 us  [to_channels(): return lax.all_to_all(parts, 'seq', split_axis=0, concat_axis=0, tiled=True)]
    all_to_all x1, waiting for transfers between devices: 7.52 us -> 10.8 us  [on_device(): lax.all_to_all(copies, 'chan', split_axis=0, concat_axis=0, tiled=True)]
    unnamed x77 -> x69, local copies, waits for them, and re-layouts: 18.8 us -> 16.5 us
    dot_general x6 -> x8, matrix products: 8.05 us -> 9.22 us  [lead_apply(): return jnp.einsum('kn,nrm->krm', table, fields, precision=TABLE_PRECISION)]
    dot_general x12 -> x16, matrix products: 14.9 us -> 15.1 us  [minor_apply(): return jnp.einsum('krm,mj->krj', fields, table, precision=TABLE_PRECISION)]
  transfers between devices with their start and end apart: 6 -> 8, of which waited for: 5 -> 7; matrix products, arithmetic and copies ran while one was open for 14% -> 16% of each run, Pallas kernels for 0% -> 0%
where the time goes in v2:
time: 286 us; the launch traced here: 284 us
  waiting for transfers between devices  152 us (53%)
  matrix products  39.4 us (14%)
  starting transfers between devices  34.1 us (12%)
  local copies, waits for them, and re-layouts  33.2 us (12%)
  between operations  14.6 us (5%)
  other arithmetic  11.1 us (4%)
    psum x1, waiting for transfers between devices, on_device(): lax.psum((grad_win, grad_wout * scale), ('seq', 'rep'))  72.5 us
    ppermute x1, waiting for transfers between devices, rep_sum(): total = total + lax.ppermute(value, 'rep', pairs)  27.2 us
    all_to_all x2, waiting for transfers between devices, to_channels(): return lax.all_to_all(parts, 'seq', split_axis=0, concat_axis=0, tiled=True)  22.6 us
    all_to_all x2, waiting for transfers between devices, to_rows(): lax.all_to_all(fields, 'seq', split_axis=0, concat_axis=0, tiled=True)  18.8 us
    unnamed x69, local copies, waits for them, and re-layouts  16.5 us
    dot_general x16, matrix products, minor_apply(): return jnp.einsum('krm,mj->krj', fields, table, precision=TABLE_PRECISION)  15.1 us
    all_to_all x2, starting transfers between devices, to_channels(): return lax.all_to_all(parts, 'seq', split_axis=0, concat_axis=0, tiled=True)  12.2 us
    all_to_all x2, starting transfers between devices, to_rows(): lax.all_to_all(fields, 'seq', split_axis=0, concat_axis=0, tiled=True)  11.3 us
  transfers between devices with their start and end apart: 8, of which 7 were waited for; matrix products, arithmetic and copies ran while one was open for 16% of the time, Pallas kernels for 0%

profile of v2, /device:TPU:6, one launch (start us, length us, event | category | flops | bytes accessed | tf_op | source)
XLA Modules:
  0.0 284.4 jit_solution(8187991732101139091)
XLA Ops:
  7.2 1.1 copy.141
  9.4 4.6 %all-to-all-start.1 = ((bf16[4,256,512]{1,2,0:T(8,128)(2,1)}), bf16[4,256,512]{1,2,0:T(8,128)(2,1)S(1)}, u32[]{:S(2)}, u32[]{:S(2)}) async-start(bf16[4,256,512]{1,2,0:T(8,128)(2,1)} %broadcast_in_dim.7), calls=%async_computation.1 | async-start | bytes 2097152 | tf_op jit(solution)/shard_map/all_to_all | solution.py:121
  15.6 2.7 copy.131
  18.2 10.8 %all-to-all-done.1 = bf16[4,256,512]{1,2,0:T(8,128)(2,1)S(1)} async-done(((bf16[4,256,512]{1,2,0:T(8,128)(2,1)}), bf16[4,256,512]{1,2,0:T(8,128)(2,1)S(1)}, u32[]{:S(2)}, u32[]{:S(2)}) %all-to-all-start.1) | async-done | bytes 1048608 | tf_op jit(solution)/shard_map/all_to_all | solution.py:121
  29.1 6.8 %all-to-all-start = ((f32[16,2,32,256]{3,2,1,0:T(8,128)}), f32[16,2,32,256]{3,2,1,0:T(8,128)}, u32[]{:S(2)}, u32[]{:S(2)}) async-start(f32[16,2,32,256]{3,2,1,0:T(8,128)} %copy.135), calls=%async_computation | async-start | bytes 2097152 | tf_op jit(solution)/shard_map/all_to_all | solution.py:83
  35.9 2.2 fusion.32
  38.1 1.5 bitcast_multiply_fusion.3
  40.7 10.6 %all-to-all-done = f32[16,2,32,256]{3,2,1,0:T(8,128)} async-done(((f32[16,2,32,256]{3,2,1,0:T(8,128)}), f32[16,2,32,256]{3,2,1,0:T(8,128)}, u32[]{:S(2)}, u32[]{:S(2)}) %all-to-all-start) | async-done | bytes 1048608 | tf_op jit(solution)/shard_map/all_to_all | solution.py:83
  51.3 5.4 %all-to-all-start.2 = ((f32[16,2,32,256]{3,2,1,0:T(8,128)}), f32[16,2,32,256]{3,2,1,0:T(8,128)}, u32[]{:S(2)}, u32[]{:S(2)}) async-start(f32[16,2,32,256]{3,2,1,0:T(8,128)} %maximum_bitcast_fusion.1), calls=%async_computation.2 | async-start | bytes 2097152 | tf_op jit(solution)/shard_map/all_to_all | solution.py:83
  56.7 1.8 copy.136
  58.5 1.5 fusion.40
  60.1 12.1 %all-to-all-done.2 = f32[16,2,32,256]{3,2,1,0:T(8,128)} async-done(((f32[16,2,32,256]{3,2,1,0:T(8,128)}), f32[16,2,32,256]{3,2,1,0:T(8,128)}, u32[]{:S(2)}, u32[]{:S(2)}) %all-to-all-start.2) | async-done | bytes 1048608 | tf_op jit(solution)/shard_map/all_to_all | solution.py:83
  72.1 1.8 copy.145
  75.9 1.1 multiply_add_fusion.3
  77.0 1.1 fusion.19
  78.1 1.1 fusion.15
  79.2 1.1 fusion.9
  80.3 1.1 fusion.13
  81.5 1.1 convolution_add_fusion.7
  82.6 1.1 convolution_add_fusion.6
  83.7 1.1 convolution_add_fusion.9
  84.9 1.3 convolution_add_fusion.8
  91.8 1.9 multiply_add_fusion
  94.8 1.1 convolution_add_fusion.1
  95.9 1.6 copy.154
  97.5 5.4 %all-to-all-start.3 = ((f32[16,2,32,256]{3,2,1,0:T(8,128)}), f32[16,2,32,256]{3,2,1,0:T(8,128)}, u32[]{:S(2)}, u32[]{:S(2)}) async-start(f32[16,2,32,256]{3,2,1,0:T(8,128)} %copy.154), calls=%async_computation.3 | async-start | bytes 2097152 | tf_op jit(solution)/shard_map/all_to_all | solution.py:88
  103.0 4.2 %copy.172 = bf16[2048,512]{1,0:T(8,128)(2,1)} copy(bf16[2048,512]{0,1:T(8,128)(2,1)} %bitcast.176) | data formatting | bytes 4194304 | tf_op jit(solution)/shard_map/dot_general | solution.py:160
  107.2 2.2 fusion.4
  111.1 1.4 fusion.21
  112.7 1.3 maximum_multiply_fusion
  114.0 1.4 collective-permute-start
  115.3 3.1 %all-to-all-done.3 = f32[16,2,32,256]{3,2,1,0:T(8,128)} async-done(((f32[16,2,32,256]{3,2,1,0:T(8,128)}), f32[16,2,32,256]{3,2,1,0:T(8,128)}, u32[]{:S(2)}, u32[]{:S(2)}) %all-to-all-start.3) | async-done | bytes 1048608 | tf_op jit(solution)/shard_map/all_to_all | solution.py:88
  118.4 1.4 fusion.39
  120.4 2.2 fusion
  122.7 2.8 convolution_multiply_fusion.1
  126.4 3.7 %convolution_bitcast_fusion = f32[4,256,512]{2,1,0:T(8,128)} fusion(bf16[4,512,512]{2,1,0:T(8,128)(2,1)} %bitcast.191, bf16[1,256,1,512]{1,3,2,0:T(8,128)(2,1)S(1)} %copy-done.15), kind=kOutput, calls=%fused_computation.3 | convolution fusion | flops 536870912 | bytes 4456448 | tf_op jit(solution)/shard_map/dot_general | solution.py:160
  130.1 4.6 %all-to-all-start.4 = ((f32[4,256,512]{2,1,0:T(8,128)}), f32[4,256,512]{2,1,0:T(8,128)}, u32[]{:S(2)}, u32[]{:S(2)}) async-start(f32[4,256,512]{2,1,0:T(8,128)} %convolution_bitcast_fusion), calls=%async_computation.4 | async-start | bytes 4194304 | tf_op jit(solution)/shard_map/all_to_all | solution.py:105
  134.7 27.2 %collective-permute-done = f32[16,3,32,256]{3,2,1,0:T(8,128)} collective-permute-done((f32[16,3,32,256]{3,2,1,0:T(8,128)}, f32[16,3,32,256]{3,2,1,0:T(8,128)}, u32[]{:S(2)}, u32[]{:S(2)}) %collective-permute-start) | collective-permute-done | bytes 1572896 | tf_op jit(solution)/shard_map/ppermute | solution.py:97
  161.9 2.9 %fusion.35 = f32[16,3,32,256]{3,2,1,0:T(8,128)} fusion(f32[16,3,32,256]{3,2,1,0:T(8,128)} %collective-permute-done, f32[16,1,32,256]{3,2,1,0:T(8,128)S(1)} %copy-done.7, f32[16,2,32,256]{3,2,1,0:T(8,128)S(1)} %copy.162), kind=kLoop, calls=%fused_computation.87 | loop fusion | flops 1179648 | bytes 4718592 | tf_op jit(solution)/shard_map/add | solution.py:97
  164.8 5.8 %all-to-all-start.5 = ((f32[16,3,32,256]{3,2,1,0:T(8,128)}), f32[16,3,32,256]{3,2,1,0:T(8,128)S(1)}, u32[]{:S(2)}, u32[]{:S(2)}) async-start(f32[16,3,32,256]{3,2,1,0:T(8,128)} %fusion.35), calls=%async_computation.5 | async-start | bytes 3145728 | tf_op jit(solution)/shard_map/all_to_all | solution.py:88
  170.7 2.8 fusion.2
  173.5 2.4 fusion.22
  175.9 15.8 %all-to-all-done.5 = f32[16,3,32,256]{3,2,1,0:T(8,128)S(1)} async-done(((f32[16,3,32,256]{3,2,1,0:T(8,128)}), f32[16,3,32,256]{3,2,1,0:T(8,128)S(1)}, u32[]{:S(2)}, u32[]{:S(2)}) %all-to-all-start.5) | async-done | bytes 1572896 | tf_op jit(solution)/shard_map/all_to_all | solution.py:88
  191.8 1.2 copy-done.5
  195.1 1.7 slice_reduce_fusion
  196.8 72.5 %all-reduce.3.cloned.1.call-done = (f32[512,1536]{0,1:T(8,128)}, f32[512,2048]{1,0:T(8,128)}) async-done(((f32[512,1536]{0,1:T(8,128)}, f32[512,2048]{1,0:T(8,128)}), (f32[512,1536]{0,1:T(8,128)}, f32[512,2048]{1,0:T(8,128)})) %all-reduce.3.cloned.1.call-update) | async-done | bytes 7340048 | tf_op jit(solution)/shard_map/psum | solution.py:177
  269.3 3.5 %copy.164 = f32[512,1536]{1,0:T(8,128)} copy(f32[512,1536]{0,1:T(8,128)} %get-tuple-element.35) | data formatting | bytes 6291456
  272.8 4.7 %copy.202 = f32[512,2048]{1,0:T(8,128)} copy(f32[512,2048]{1,0:T(8,128)} %get-tuple-element.79) | data formatting | bytes 8388608
  (95 shorter events, 17.9 us)
Async XLA Ops:
  7.2 28.7 %copy-start = (bf16[1,256,512]{2,1,0:T(8,128)(2,1)S(1)}, bf16[1,256,512]{2,1,0:T(8,128)(2,1)}, u32[]{:S(2)}) copy-start(bf16[1,256,512]{2,1,0:T(8,128)(2,1)} %param.31) | copy-start | bytes 786436
  8.3 5.7 %copy-start.22 = (f32[256,512]{1,0:T(8,128)S(1)}, f32[256,512]{1,0:T(8,128)}, u32[]{:S(2)}) copy-start(f32[256,512]{1,0:T(8,128)} %param.34) | copy-start | bytes 1572868
  9.4 4.8 %copy-start.23 = (f32[256,512]{1,0:T(8,128)S(1)}, f32[256,512]{1,0:T(8,128)}, u32[]{:S(2)}) copy-start(f32[256,512]{1,0:T(8,128)} %param.35) | copy-start | bytes 1572868
  9.4 19.7 %all-to-all-start.1 = ((bf16[4,256,512]{1,2,0:T(8,128)(2,1)}), bf16[4,256,512]{1,2,0:T(8,128)(2,1)S(1)}, u32[]{:S(2)}, u32[]{:S(2)}) async-start(bf16[4,256,512]{1,2,0:T(8,128)(2,1)} %broadcast_in_dim.7), calls=%async_computation.1 | async-start | bytes 2097152 | tf_op jit(solution)/shard_map/all_to_all | solution.py:121
  29.1 9.1 %copy-start.3 = (bf16[4,256,512]{1,2,0:T(8,128)(2,1)}, bf16[4,256,512]{1,2,0:T(8,128)(2,1)S(1)}, u32[]{:S(2)}) copy-start(bf16[4,256,512]{1,2,0:T(8,128)(2,1)S(1)} %all-to-all-done.1) | copy-start | bytes 3145732
  29.1 22.2 %all-to-all-start = ((f32[16,2,32,256]{3,2,1,0:T(8,128)}), f32[16,2,32,256]{3,2,1,0:T(8,128)}, u32[]{:S(2)}, u32[]{:S(2)}) async-start(f32[16,2,32,256]{3,2,1,0:T(8,128)} %copy.135), calls=%async_computation | async-start | bytes 2097152 | tf_op jit(solution)/shard_map/all_to_all | solution.py:83
  35.9 2.3 copy-start.2
  38.1 1.5 copy-start.8
  51.3 20.9 %all-to-all-start.2 = ((f32[16,2,32,256]{3,2,1,0:T(8,128)}), f32[16,2,32,256]{3,2,1,0:T(8,128)}, u32[]{:S(2)}, u32[]{:S(2)}) async-start(f32[16,2,32,256]{3,2,1,0:T(8,128)} %maximum_bitcast_fusion.1), calls=%async_computation.2 | async-start | bytes 2097152 | tf_op jit(solution)/shard_map/all_to_all | solution.py:83
  56.7 1.9 copy-start.24
  74.0 0.7 copy-start.25
  74.7 1.2 copy-start.10
  74.7 1.2 copy-start.28
  74.7 1.2 copy-start.29
  75.9 1.1 copy-start.1
  80.3 1.1 copy-start.12
  82.6 1.1 copy-start.11
  91.1 0.7 copy-start.26
  91.1 0.7 copy-start.27
  97.5 20.9 %all-to-all-start.3 = ((f32[16,2,32,256]{3,2,1,0:T(8,128)}), f32[16,2,32,256]{3,2,1,0:T(8,128)}, u32[]{:S(2)}, u32[]{:S(2)}) async-start(f32[16,2,32,256]{3,2,1,0:T(8,128)} %copy.154), calls=%async_computation.3 | async-start | bytes 2097152 | tf_op jit(solution)/shard_map/all_to_all | solution.py:88
  103.0 166.3 %all-reduce.3.cloned.1.call-start = ((), (), s32[]{:S(2)}) async-start(), calls=%async_computation.6 | async-start | bytes 14680064 | tf_op jit(solution)/shard_map/psum | solution.py:177
  112.6 1.3 copy-start.6
  114.0 5.8 %copy-start.30 = (f32[512]{0:T(512)S(1)}, f32[512]{0:T(512)}, u32[]{:S(2)}) copy-start(f32[512]{0:T(512)} %param.36) | copy-start | bytes 6148
  114.0 48.0 %collective-permute-start = (f32[16,3,32,256]{3,2,1,0:T(8,128)}, f32[16,3,32,256]{3,2,1,0:T(8,128)}, u32[]{:S(2)}, u32[]{:S(2)}) collective-permute-start(f32[16,3,32,256]{3,2,1,0:T(8,128)} %maximum_multiply_fusion), channel_id=1, source_target_pairs={{0,1},{1,0},{2,3},{3,2},{4,5},{5,4},{6,7},{7,6},{8,9},{9,8},{10,11... | collective-permute-start | bytes 4718600 | tf_op jit(solution)/shard_map/ppermute | solution.py:97
  118.4 1.4 copy-start.9
  118.4 1.6 copy-start.13
  120.0 2.7 copy-start.14
  120.3 2.4 copy-start.16
  120.3 2.4 copy-start.18
  120.3 2.4 copy-start.20
  120.4 2.3 copy-start.4
  125.4 0.9 copy-start.15
  130.1 31.9 %copy-start.7 = (f32[16,1,32,256]{3,2,1,0:T(8,128)S(1)}, f32[16,1,32,256]{3,2,1,0:T(8,128)}, u32[]{:S(2)}) copy-start(f32[16,1,32,256]{3,2,1,0:T(8,128)} %copy-done.6) | copy-start | bytes 1572868
  130.1 34.8 %all-to-all-start.4 = ((f32[4,256,512]{2,1,0:T(8,128)}), f32[4,256,512]{2,1,0:T(8,128)}, u32[]{:S(2)}, u32[]{:S(2)}) async-start(f32[4,256,512]{2,1,0:T(8,128)} %convolution_bitcast_fusion), calls=%async_computation.4 | async-start | bytes 4194304 | tf_op jit(solution)/shard_map/all_to_all | solution.py:105
  164.8 5.9 %copy-start.17 = (bf16[1,256,512]{1,2,0:T(8,128)(2,1)S(1)}, bf16[1,256,512]{1,2,0:T(8,128)(2,1)}, u32[]{:S(2)}) copy-start(bf16[1,256,512]{1,2,0:T(8,128)(2,1)} %copy-done.16) | copy-start | bytes 786436
  164.8 5.9 %copy-start.19 = (bf16[256,512]{0,1:T(8,128)(2,1)S(1)}, bf16[256,512]{0,1:T(8,128)(2,1)}, u32[]{:S(2)}) copy-start(bf16[256,512]{0,1:T(8,128)(2,1)} %copy-done.18) | copy-start | bytes 786436
  164.8 5.9 %copy-start.21 = (bf16[1,256,512]{1,2,0:T(8,128)(2,1)S(1)}, bf16[1,256,512]{1,2,0:T(8,128)(2,1)}, u32[]{:S(2)}) copy-start(bf16[1,256,512]{1,2,0:T(8,128)(2,1)} %copy-done.20) | copy-start | bytes 786436
  164.8 26.8 %all-to-all-start.5 = ((f32[16,3,32,256]{3,2,1,0:T(8,128)}), f32[16,3,32,256]{3,2,1,0:T(8,128)S(1)}, u32[]{:S(2)}, u32[]{:S(2)}) async-start(f32[16,3,32,256]{3,2,1,0:T(8,128)} %fusion.35), calls=%async_computation.5 | async-start | bytes 3145728 | tf_op jit(solution)/shard_map/all_to_all | solution.py:88
  191.8 1.2 copy-start.5
Sparse Core Ops, SparseCore 0:
  125.6 143.6 all-reduce.2

commit v3 on v1

--- a/solution.py
+++ b/solution.py
@@ -136,7 +136,6 @@
     gain_re = spec_re[:, 1] + spec_re[:, 2]
     gain_im = spec_im[:, 1] - spec_im[:, 2]
     grad_re, grad_im = (spec_re[:, 3], spec_im[:, 3])
-    grad_cs = spread[:, 3:]
     joint_re, joint_im = complex_product(gain_re, gain_im, mix_re, mix_im)
     back_re, back_im = complex_product(gain_re, -gain_im, grad_re, grad_im)
     both = to_rows(
@@ -151,9 +150,7 @@
         jnp.stack([cross_re, cross_re], axis=1), jnp.stack([cross_im, -cross_im], axis=1)
     )
     scale = 1.0 / math.sqrt(lax.axis_size("rep") * lax.axis_size("seq") * row_count)
-    skip_part = jnp.sum(grad_cs * spread[:, :1], axis=(0, 3))
-    skip_field = jnp.broadcast_to(skip_part[None, :, :, None], grad_cs.shape)
-    filt_grads = to_rows(rep_sum(jnp.concatenate([cross, skip_field], axis=1) * scale))
+    filt_grads = to_rows(rep_sum(cross * scale))
     conv_out = long_conv + skip_gain * mixed
     gated = (queries * conv_out).astype(jnp.bfloat16)
     out_terms = jnp.dot(gated, w_out, preferred_element_type=jnp.float32)
@@ -173,15 +170,19 @@
         "mni,smnj->nisj", input_blocks, pre_blocks, preferred_element_type=jnp.float32
     )
     grad_win = grad_win.reshape(chan_width, 3 * BLOCK) * scale
-    grad_win, grad_wout = lax.psum((grad_win, grad_wout * scale), ("seq", "rep"))
+    grad_skip = jnp.sum(grad_conv * mixed, axis=0)
+    out_width = grad_wout.shape[1]
+    skip_row = jnp.pad(grad_skip, (0, out_width - chan_width))[None]
+    joined = jnp.concatenate([grad_wout, skip_row], axis=0) * scale
+    grad_win, joined = lax.psum((grad_win, joined), ("seq", "rep"))
     return (
         layer_out[None],
         d_input[None],
         grad_win,
-        grad_wout,
+        joined[:chan_width],
         filt_grads[0],
         filt_grads[1],
-        filt_grads[2, 0],
+        joined[chan_width, :chan_width],
     )
 
 

time: 278 us -> 266 us (0.957)
  waiting for transfers between devices: 127 us -> 118 us
  local copies, waits for them, and re-layouts: 32.3 us -> 29.3 us
    all_to_all x1, waiting for transfers between devices: 0.01 us -> 22.4 us  [chan_reduce_scatter(): lax.all_to_all(pieces, 'chan', split_axis=0, concat_axis=0, tiled=True)]
    psum x1, waiting for transfers between devices: 72.5 us -> 53.6 us  [on_device(): grad_win, joined = lax.psum((grad_win, joined), ('seq', 'rep'))]
    ppermute x1, waiting for transfers between devices: 27.7 us -> 15.3 us  [rep_sum(): total = total + lax.ppermute(value, 'rep', pairs)]
    unnamed x77 -> x62, local copies, waits for them, and re-layouts: 18.8 us -> 10.9 us
    slice x1 -> x2, local copies, waits for them, and re-layouts: 1.73 us -> 5.99 us  [the longest x1 4.7 us: on_device(): joined[:chan_width]]
  transfers between devices with their start and end apart: 6 -> 6, of which waited for: 5 -> 6; matrix products, arithmetic and copies ran while one was open for 14% -> 14% of each run, Pallas kernels for 0% -> 0%
where the time goes in v3:
time: 266 us; the launch traced here: 265 us
  waiting for transfers between devices  118 us (44%)
  matrix products  37 us (14%)
  blocking collectives  33.1 us (12%)
  local copies, waits for them, and re-layouts  29.3 us (11%)
  starting transfers between devices  21.8 us (8%)
  between operations  14.6 us (5%)
  other arithmetic  10.9 us (4%)
    psum x1, waiting for transfers between devices, on_device(): grad_win, joined = lax.psum((grad_win, joined), ('seq', 'rep'))  53.6 us
    all_to_all x1, blocking collectives, to_channels(): return lax.all_to_all(parts, 'seq', split_axis=0, concat_axis=0, tiled=True)  33.1 us
    all_to_all x1, waiting for transfers between devices, chan_reduce_scatter(): lax.all_to_all(pieces, 'chan', split_axis=0, concat_axis=0, tiled=True)  22.4 us
    all_to_all x2, waiting for transfers between devices, to_rows(): lax.all_to_all(fields, 'seq', split_axis=0, concat_axis=0, tiled=True)  19.4 us
    ppermute x1, waiting for transfers between devices, rep_sum(): total = total + lax.ppermute(value, 'rep', pairs)  15.3 us
    dot_general x12, matrix products, minor_apply(): return jnp.einsum('krm,mj->krj', fields, table, precision=TABLE_PRECISION)  14.6 us
    all_to_all x2, starting transfers between devices, to_rows(): lax.all_to_all(fields, 'seq', split_axis=0, concat_axis=0, tiled=True)  11 us
    unnamed x62, local copies, waits for them, and re-layouts  10.9 us
  transfers between devices with their start and end apart: 6, of which 6 were waited for; matrix products, arithmetic and copies ran while one was open for 14% of the time, Pallas kernels for 0%

profile of v3, /device:TPU:6, one launch (start us, length us, event | category | flops | bytes accessed | tf_op | source)
XLA Modules:
  0.0 265.1 jit_solution(13492796637696332359)
XLA Ops:
  7.2 1.2 copy.91
  8.4 1.0 broadcast_in_dim.7
  9.4 4.6 %all-to-all-start = ((bf16[4,256,512]{1,2,0:T(8,128)(2,1)}), bf16[4,256,512]{1,2,0:T(8,128)(2,1)S(1)}, u32[]{:S(2)}, u32[]{:S(2)}) async-start(bf16[4,256,512]{1,2,0:T(8,128)(2,1)} %broadcast_in_dim.7), calls=%async_computation | async-start | bytes 2097152 | tf_op jit(solution)/shard_map/all_to_all | solution.py:121
  14.0 1.0 copy.89
  15.0 2.0 copy.90
  17.0 1.6 copy.85
  18.6 2.0 fusion.34
  20.6 0.9 bitcast_multiply_fusion.4
  21.5 7.6 %all-to-all-done = bf16[4,256,512]{1,2,0:T(8,128)(2,1)S(1)} async-done(((bf16[4,256,512]{1,2,0:T(8,128)(2,1)}), bf16[4,256,512]{1,2,0:T(8,128)(2,1)S(1)}, u32[]{:S(2)}, u32[]{:S(2)}) %all-to-all-start) | async-done | bytes 1048608 | tf_op jit(solution)/shard_map/all_to_all | solution.py:121
  29.1 3.5 %multiply_reduce_fusion = (f32[512]{0:T(512)S(1)}, f32[256,512]{0,1:T(8,128)S(1)}, f32[256,512]{0,1:T(8,128)}) fusion(f32[3,256,1,512]{1,3,0,2:T(8,128)S(1)} %bitcast.163, f32[3,256,1,512]{1,3,2,0:T(8,128)S(1)} %bitcast.164, bf16[512,2048]{1,0:T(8,128)(2,1)} %param.27, bf16[256,2048]{0,1:T(8,128)(2,1)S(1)} %bitcast.178), kind=kOutput, calls=%fused_computation.62 | convolution fusion | flops 537394688 | bytes 5769216 | tf_op jit(solution)/shard_map/dot_general | solution.py:129
  33.1 33.1 %all_to_all.25 = f32[16,4,32,256]{3,2,1,0:T(8,128)S(1)} all-to-all(f32[16,4,32,256]{3,2,1,0:T(8,128)S(1)} %copy.93), channel_id=1, replica_groups=mesh['seq'=16,'chan'=4,'rep'=2] {'seq'}, dimensions={0} | all-to-all | bytes 4194304 | tf_op jit(solution)/shard_map/all_to_all | solution.py:83
  66.2 1.2 copy.94
  67.5 1.0 fusion.40
  68.6 1.4 multiply_add_fusion
  70.0 2.1 fusion.1
  72.1 2.1 fusion.3
  74.2 2.1 fusion.9
  76.3 2.3 fusion.12
  78.6 0.8 fusion.37
  84.6 1.9 multiply_add_fusion.1
  86.5 1.1 fusion.22
  87.5 1.1 convolution_add_fusion.1
  88.7 1.6 copy.101
  90.3 5.3 %all-to-all-start.2 = ((f32[16,2,32,256]{3,2,1,0:T(8,128)}), f32[16,2,32,256]{3,2,1,0:T(8,128)}, u32[]{:S(2)}, u32[]{:S(2)}) async-start(f32[16,2,32,256]{3,2,1,0:T(8,128)} %copy.101), calls=%async_computation.2 | async-start | bytes 2097152 | tf_op jit(solution)/shard_map/all_to_all | solution.py:88
  95.9 1.1 fusion.19
  97.0 2.3 fusion.15
  99.2 1.6 copy.110
  100.8 1.4 collective-permute-start
  102.2 8.8 %all-to-all-done.2 = f32[16,2,32,256]{3,2,1,0:T(8,128)} async-done(((f32[16,2,32,256]{3,2,1,0:T(8,128)}), f32[16,2,32,256]{3,2,1,0:T(8,128)}, u32[]{:S(2)}, u32[]{:S(2)}) %all-to-all-start.2) | async-done | bytes 1048608 | tf_op jit(solution)/shard_map/all_to_all | solution.py:88
  111.0 1.4 fusion.39
  114.3 2.2 fusion
  116.5 2.5 maximum_multiply_fusion
  119.0 15.3 %collective-permute-done = f32[16,2,32,256]{3,2,1,0:T(8,128)} collective-permute-done((f32[16,2,32,256]{3,2,1,0:T(8,128)}, f32[16,2,32,256]{3,2,1,0:T(8,128)}, u32[]{:S(2)}, u32[]{:S(2)}) %collective-permute-start) | collective-permute-done | bytes 1048608 | tf_op jit(solution)/shard_map/ppermute | solution.py:97
  134.4 2.9 %copy_add_fusion = f32[16,2,32,256]{3,2,1,0:T(8,128)} fusion(f32[16,2,32,256]{3,2,1,0:T(8,128)} %collective-permute-done, f32[16,2,32,256]{3,0,2,1:T(8,128)S(1)} %bitcast.173), kind=kLoop, calls=%fused_computation.76 | loop fusion | flops 262144 | bytes 3145728 | tf_op jit(solution)/shard_map/add | solution.py:97
  137.3 5.7 %all-to-all-start.4 = ((f32[16,2,32,256]{3,2,1,0:T(8,128)}), f32[16,2,32,256]{3,2,1,0:T(8,128)S(1)}, u32[]{:S(2)}, u32[]{:S(2)}) async-start(f32[16,2,32,256]{3,2,1,0:T(8,128)} %copy_add_fusion), calls=%async_computation.4 | async-start | bytes 2097152 | tf_op jit(solution)/shard_map/all_to_all | solution.py:88
  143.0 4.0 %copy.120 = bf16[2048,512]{1,0:T(8,128)(2,1)} copy(bf16[2048,512]{0,1:T(8,128)(2,1)} %bitcast.184) | data formatting | bytes 4194304 | tf_op jit(solution)/shard_map/dot_general | solution.py:156
  147.0 3.7 %convolution_bitcast_fusion = f32[4,256,512]{2,1,0:T(8,128)} fusion(bf16[4,512,512]{2,1,0:T(8,128)(2,1)} %bitcast.185, bf16[1,256,1,512]{1,3,2,0:T(8,128)(2,1)S(1)} %copy-done.10), kind=kOutput, calls=%fused_computation.16 | convolution fusion | flops 536870912 | bytes 4456448 | tf_op jit(solution)/shard_map/dot_general | solution.py:156
  150.7 10.6 %all-to-all-done.4 = f32[16,2,32,256]{3,2,1,0:T(8,128)S(1)} async-done(((f32[16,2,32,256]{3,2,1,0:T(8,128)}), f32[16,2,32,256]{3,2,1,0:T(8,128)S(1)}, u32[]{:S(2)}, u32[]{:S(2)}) %all-to-all-start.4) | async-done | bytes 1048608 | tf_op jit(solution)/shard_map/all_to_all | solution.py:88
  161.3 4.5 %all-to-all-start.3 = ((f32[4,256,512]{2,1,0:T(8,128)}), f32[4,256,512]{2,1,0:T(8,128)}, u32[]{:S(2)}, u32[]{:S(2)}) async-start(f32[4,256,512]{2,1,0:T(8,128)} %convolution_bitcast_fusion), calls=%async_computation.3 | async-start | bytes 4194304 | tf_op jit(solution)/shard_map/all_to_all | solution.py:105
  165.9 2.3 fusion.17
  168.3 1.0 copy.114
  169.3 1.0 copy.113
  170.3 22.4 %all-to-all-done.3 = f32[4,256,512]{2,1,0:T(8,128)} async-done(((f32[4,256,512]{2,1,0:T(8,128)}), f32[4,256,512]{2,1,0:T(8,128)}, u32[]{:S(2)}, u32[]{:S(2)}) %all-to-all-start.3) | async-done | bytes 2097184 | tf_op jit(solution)/shard_map/all_to_all | solution.py:105
  192.7 2.4 fusion.24
  195.1 53.6 %all-reduce.4.cloned.1.call-done = (f32[512,1536]{0,1:T(8,128)}, f32[513,2048]{1,0:T(8,128)}) async-done(((f32[512,1536]{0,1:T(8,128)}, f32[513,2048]{1,0:T(8,128)}), (f32[512,1536]{0,1:T(8,128)}, f32[513,2048]{1,0:T(8,128)})) %all-reduce.4.cloned.1.call-update) | async-done | bytes 7348240 | tf_op jit(solution)/shard_map/psum | solution.py:177
  248.7 1.3 slice.111
  250.0 4.7 %slice.108 = f32[512,2048]{1,0:T(8,128)} slice(f32[513,2048]{1,0:T(8,128)} %get-tuple-element.29), slice={[0:512], [0:2048]} | slice | bytes 8388608 | tf_op jit(solution)/shard_map/slice | solution.py:182
  254.7 3.5 %copy.112 = f32[512,1536]{1,0:T(8,128)} copy(f32[512,1536]{0,1:T(8,128)} %get-tuple-element.28) | data formatting | bytes 6291456
  (78 shorter events, 7.9 us)
Async XLA Ops:
  7.2 11.4 %copy-start = (bf16[1,256,512]{2,1,0:T(8,128)(2,1)S(1)}, bf16[1,256,512]{2,1,0:T(8,128)(2,1)}, u32[]{:S(2)}) copy-start(bf16[1,256,512]{2,1,0:T(8,128)(2,1)} %param.25) | copy-start | bytes 786436
  7.2 6.8 %copy-start.20 = (f32[256,512]{1,0:T(8,128)S(1)}, f32[256,512]{1,0:T(8,128)}, u32[]{:S(2)}) copy-start(f32[256,512]{1,0:T(8,128)} %param.28) | copy-start | bytes 1572868
  9.4 7.6 %copy-start.14 = (bf16[512,1536]{1,0:T(8,128)(2,1)S(1)}, bf16[512,1536]{1,0:T(8,128)(2,1)}, u32[]{:S(2)}) copy-start(bf16[512,1536]{1,0:T(8,128)(2,1)} %param.26) | copy-start | bytes 4718596
  9.4 19.7 %all-to-all-start = ((bf16[4,256,512]{1,2,0:T(8,128)(2,1)}), bf16[4,256,512]{1,2,0:T(8,128)(2,1)S(1)}, u32[]{:S(2)}, u32[]{:S(2)}) async-start(bf16[4,256,512]{1,2,0:T(8,128)(2,1)} %broadcast_in_dim.7), calls=%async_computation | async-start | bytes 2097152 | tf_op jit(solution)/shard_map/all_to_all | solution.py:121
  29.1 3.5 %copy-start.2 = (bf16[4,256,512]{1,2,0:T(8,128)(2,1)}, bf16[4,256,512]{1,2,0:T(8,128)(2,1)S(1)}, u32[]{:S(2)}) copy-start(bf16[4,256,512]{1,2,0:T(8,128)(2,1)S(1)} %all-to-all-done) | copy-start | bytes 3145732
  29.1 3.5 %copy-start.5 = (f32[1,256,1,512]{1,3,2,0:T(8,128)S(1)}, f32[1,256,1,512]{1,3,2,0:T(8,128)}, u32[]{:S(2)}) copy-start(f32[1,256,1,512]{1,3,2,0:T(8,128)} %bitcast_multiply_fusion.4) | copy-start | bytes 1572868
  29.1 3.5 %copy-start.12 = (f32[256,512]{0,1:T(8,128)S(1)}, f32[256,512]{0,1:T(8,128)}, u32[]{:S(2)}) copy-start(f32[256,512]{0,1:T(8,128)} %copy.89) | copy-start | bytes 1572868
  29.1 3.5 %copy-start.13 = (f32[256,512]{0,1:T(8,128)S(1)}, f32[256,512]{0,1:T(8,128)}, u32[]{:S(2)}) copy-start(f32[256,512]{0,1:T(8,128)} %copy.90) | copy-start | bytes 1572868
  66.2 1.2 copy-start.21
  67.5 1.1 copy-start.22
  67.5 1.1 copy-start.25
  67.5 1.1 copy-start.26
  68.6 1.5 copy-start.1
  70.0 2.1 copy-start.7
  74.2 2.1 copy-start.8
  83.8 0.7 copy-start.23
  83.8 0.7 copy-start.24
  90.3 20.8 %all-to-all-start.2 = ((f32[16,2,32,256]{3,2,1,0:T(8,128)}), f32[16,2,32,256]{3,2,1,0:T(8,128)}, u32[]{:S(2)}, u32[]{:S(2)}) async-start(f32[16,2,32,256]{3,2,1,0:T(8,128)} %copy.101), calls=%async_computation.2 | async-start | bytes 2097152 | tf_op jit(solution)/shard_map/all_to_all | solution.py:88
  95.6 153.1 %all-reduce.4.cloned.1.call-start = ((), (), s32[]{:S(2)}) async-start(), calls=%async_computation.5 | async-start | bytes 14811136 | tf_op jit(solution)/shard_map/psum | solution.py:177
  99.2 13.2 %copy-start.27 = (f32[512]{0:T(512)S(1)}, f32[512]{0:T(512)}, u32[]{:S(2)}) copy-start(f32[512]{0:T(512)} %param.30) | copy-start | bytes 6148
  100.8 33.6 %collective-permute-start = (f32[16,2,32,256]{3,2,1,0:T(8,128)}, f32[16,2,32,256]{3,2,1,0:T(8,128)}, u32[]{:S(2)}, u32[]{:S(2)}) collective-permute-start(f32[16,2,32,256]{3,2,1,0:T(8,128)} %copy.110), channel_id=1, source_target_pairs={{0,1},{1,0},{2,3},{3,2},{4,5},{5,4},{6,7},{7,6},{8,9},{9,8},{10,11... | collective-permute-start | bytes 3145736 | tf_op jit(solution)/shard_map/ppermute | solution.py:97
  111.0 1.4 copy-start.6
  111.0 1.7 copy-start.3
  112.7 0.7 copy-start.9
  112.7 1.1 copy-start.11
  114.2 2.4 copy-start.15
  114.2 2.4 copy-start.17
  114.2 2.3 copy-start.19
  137.3 24.1 %all-to-all-start.4 = ((f32[16,2,32,256]{3,2,1,0:T(8,128)}), f32[16,2,32,256]{3,2,1,0:T(8,128)S(1)}, u32[]{:S(2)}, u32[]{:S(2)}) async-start(f32[16,2,32,256]{3,2,1,0:T(8,128)} %copy_add_fusion), calls=%async_computation.4 | async-start | bytes 2097152 | tf_op jit(solution)/shard_map/all_to_all | solution.py:88
  143.0 4.0 %copy-start.10 = (bf16[1,256,1,512]{1,3,2,0:T(8,128)(2,1)S(1)}, bf16[1,256,1,512]{1,3,2,0:T(8,128)(2,1)}, u32[]{:S(2)}) copy-start(bf16[1,256,1,512]{1,3,2,0:T(8,128)(2,1)} %copy-done.9) | copy-start | bytes 786436
  150.7 15.1 %copy-start.4 = (bf16[512,1536]{0,1:T(8,128)(2,1)S(1)}, bf16[512,1536]{0,1:T(8,128)(2,1)}, u32[]{:S(2)}) copy-start(bf16[512,1536]{0,1:T(8,128)(2,1)} %copy.85) | copy-start | bytes 4718596
  150.7 15.1 %copy-start.16 = (bf16[1,256,512]{1,2,0:T(8,128)(2,1)S(1)}, bf16[1,256,512]{1,2,0:T(8,128)(2,1)}, u32[]{:S(2)}) copy-start(bf16[1,256,512]{1,2,0:T(8,128)(2,1)} %copy-done.15) | copy-start | bytes 786436
  150.7 15.1 %copy-start.18 = (bf16[256,512]{0,1:T(8,128)(2,1)S(1)}, bf16[256,512]{0,1:T(8,128)(2,1)}, u32[]{:S(2)}) copy-start(bf16[256,512]{0,1:T(8,128)(2,1)} %copy-done.17) | copy-start | bytes 786436
  161.3 31.4 %all-to-all-start.3 = ((f32[4,256,512]{2,1,0:T(8,128)}), f32[4,256,512]{2,1,0:T(8,128)}, u32[]{:S(2)}, u32[]{:S(2)}) async-start(f32[4,256,512]{2,1,0:T(8,128)} %convolution_bitcast_fusion), calls=%async_computation.3 | async-start | bytes 4194304 | tf_op jit(solution)/shard_map/all_to_all | solution.py:105
Sparse Core Ops, SparseCore 0:
  119.2 129.4 all-reduce.3

commit v4 on v3

--- a/solution.py
+++ b/solution.py
@@ -117,8 +117,13 @@
     w_blocks = w_in.reshape(block_count, BLOCK, 3, BLOCK)
     grad_rows = cotangent[0]
     chan_count = lax.axis_size("chan")
-    copies = jnp.broadcast_to(grad_rows[None], (chan_count,) + grad_rows.shape)
-    gathered = lax.all_to_all(copies, "chan", split_axis=0, concat_axis=0, tiled=True)
+    shifted = [grad_rows]
+    for shift in range(1, chan_count):
+        pairs = [(i, (i + shift) % chan_count) for i in range(chan_count)]
+        shifted.append(lax.ppermute(grad_rows, "chan", pairs))
+    chan_index = lax.axis_index("chan")
+    order = (chan_index - jnp.arange(chan_count, dtype=jnp.int32)) % chan_count
+    gathered = jnp.take(jnp.stack(shifted), order, axis=0)
     piece = gathered.transpose(1, 0, 2).reshape(grad_rows.shape[0], -1)
     projected = jnp.einsum(
         "mni,nisj->smnj", input_blocks, w_blocks, preferred_element_type=jnp.float32
@@ -130,12 +135,12 @@
         piece, w_out, (((1,), (1,)), ((), ())), preferred_element_type=jnp.float32
     )
     grad_conv = grad_gated * queries
-    spread = to_channels(jnp.stack([mixed, filt_fwd, filt_bwd, grad_conv]))
-    spec_re, spec_im = real_spectrum(spread)
+    spec_re, spec_im = real_spectrum(to_channels(jnp.stack([mixed, filt_fwd, filt_bwd])))
     mix_re, mix_im = (spec_re[:, 0], spec_im[:, 0])
     gain_re = spec_re[:, 1] + spec_re[:, 2]
     gain_im = spec_im[:, 1] - spec_im[:, 2]
-    grad_re, grad_im = (spec_re[:, 3], spec_im[:, 3])
+    grad_re, grad_im = real_spectrum(to_channels(grad_conv[None]))
+    grad_re, grad_im = (grad_re[:, 0], grad_im[:, 0])
     joint_re, joint_im = complex_product(gain_re, gain_im, mix_re, mix_im)
     back_re, back_im = complex_product(gain_re, -gain_im, grad_re, grad_im)
     both = to_rows(

time: 266 us -> 283 us (1.064); the launches traced: 265 us -> 278 us
  blocking collectives: 33.1 us -> 0 us
  waiting for transfers between devices: 118 us -> 140 us
  starting transfers between devices: 21.8 us -> 34.4 us
  local copies, waits for them, and re-layouts: 29.3 us -> 35.7 us
  other arithmetic: 10.9 us -> 13.9 us
    all_to_all x1 -> x0, blocking collectives: 33.1 us -> none  [to_channels(): return lax.all_to_all(parts, 'seq', split_axis=0, concat_axis=0, tiled=True)]
    all_to_all x1 -> x2, waiting for transfers between devices: 7.61 us -> 19.1 us  [to_channels(): return lax.all_to_all(parts, 'seq', split_axis=0, concat_axis=0, tiled=True)]
    ppermute x0 -> x3, waiting for transfers between devices: none -> 10.7 us  [on_device(): shifted.append(lax.ppermute(grad_rows, 'chan', pairs))]
    all_to_all x1 -> x2, starting transfers between devices: 4.59 us -> 12.4 us  [to_channels(): return lax.all_to_all(parts, 'seq', split_axis=0, concat_axis=0, tiled=True)]
    ppermute x0 -> x3, starting transfers between devices: none -> 4.68 us  [on_device(): shifted.append(lax.ppermute(grad_rows, 'chan', pairs))]
    unnamed x62 -> x68, local copies, waits for them, and re-layouts: 10.9 us -> 13.7 us
    dot_general x12 -> x16, matrix products: 14.6 us -> 16.9 us  [minor_apply(): return jnp.einsum('krm,mj->krj', fields, table, precision=TABLE_PRECISION)]
    dot_general x6 -> x8, matrix products: 7.99 us -> 8.56 us  [lead_apply(): return jnp.einsum('kn,nrm->krm', table, fields, precision=TABLE_PRECISION)]
  transfers between devices with their start and end apart: 6 -> 10, of which waited for: 6 -> 9; matrix products, arithmetic and copies ran while one was open for 14% -> 15% of each run, Pallas kernels for 0% -> 0%
where the time goes in v4:
time: 283 us; the launch traced here: 278 us
  waiting for transfers between devices  140 us (49%)
  matrix products  38.7 us (14%)
  local copies, waits for them, and re-layouts  35.7 us (13%)
  starting transfers between devices  34.4 us (12%)
  between operations  15.1 us (5%)
  other arithmetic  13.9 us (5%)
    psum x1, waiting for transfers between devices, on_device(): grad_win, joined = lax.psum((grad_win, joined), ('seq', 'rep'))  53.2 us
    all_to_all x1, waiting for transfers between devices, chan_reduce_scatter(): lax.all_to_all(pieces, 'chan', split_axis=0, concat_axis=0, tiled=True)  22.5 us
    all_to_all x2, waiting for transfers between devices, to_rows(): lax.all_to_all(fields, 'seq', split_axis=0, concat_axis=0, tiled=True)  20.5 us
    all_to_all x2, waiting for transfers between devices, to_channels(): return lax.all_to_all(parts, 'seq', split_axis=0, concat_axis=0, tiled=True)  19.1 us
    dot_general x16, matrix products, minor_apply(): return jnp.einsum('krm,mj->krj', fields, table, precision=TABLE_PRECISION)  16.9 us
    ppermute x1, waiting for transfers between devices, rep_sum(): total = total + lax.ppermute(value, 'rep', pairs)  14.3 us
    unnamed x68, local copies, waits for them, and re-layouts  13.7 us
    all_to_all x2, starting transfers between devices, to_channels(): return lax.all_to_all(parts, 'seq', split_axis=0, concat_axis=0, tiled=True)  12.4 us
  transfers between devices with their start and end apart: 10, of which 9 were waited for; matrix products, arithmetic and copies ran while one was open for 15% of the time, Pallas kernels for 0%

profile of v4, /device:TPU:6, one launch (start us, length us, event | category | flops | bytes accessed | tf_op | source)
XLA Modules:
  0.0 278.1 jit_solution(7385023728543827676)
XLA Ops:
  7.2 3.1 %collective-permute-start.2 = (bf16[256,512]{1,0:T(8,128)(2,1)}, bf16[256,512]{1,0:T(8,128)(2,1)}, u32[]{:S(2)}, u32[]{:S(2)}) collective-permute-start(bf16[256,512]{1,0:T(8,128)(2,1)} %bitcast.308), channel_id=1, source_target_pairs={{0,6},{2,0},{4,2},{6,4},{1,7},{3,1},{5,3},{7,5},{8,14},{10,8},{12,... | collective-permute-start | bytes 786440 | tf_op jit(solution)/shard_map/ppermute | solution.py:123
  11.9 1.7 copy.159
  14.8 7.0 %collective-permute-done.2 = bf16[256,512]{1,0:T(8,128)(2,1)} collective-permute-done((bf16[256,512]{1,0:T(8,128)(2,1)}, bf16[256,512]{1,0:T(8,128)(2,1)}, u32[]{:S(2)}, u32[]{:S(2)}) %collective-permute-start.2) | collective-permute-done | bytes 262176 | tf_op jit(solution)/shard_map/ppermute | solution.py:123
  21.8 3.7 %collective-permute-done = bf16[256,512]{1,0:T(8,128)(2,1)} collective-permute-done((bf16[256,512]{1,0:T(8,128)(2,1)}, bf16[256,512]{1,0:T(8,128)(2,1)}, u32[]{:S(2)}, u32[]{:S(2)}) %collective-permute-start) | collective-permute-done | bytes 262176 | tf_op jit(solution)/shard_map/ppermute | solution.py:123
  25.5 2.2 pad_maximum_fusion
  27.7 1.8 gather_fusion
  29.5 1.1 select_bitcast_fusion
  30.7 1.5 copy.177
  32.2 3.7 %multiply_reduce_fusion = (f32[512]{0:T(512)S(1)}, f32[256,512]{0,1:T(8,128)}, f32[256,512]{0,1:T(8,128)}) fusion(f32[3,256,1,512]{1,3,0,2:T(8,128)S(1)} %bitcast.265, f32[3,256,1,512]{1,3,2,0:T(8,128)S(1)} %bitcast.266, bf16[512,2048]{1,0:T(8,128)(2,1)} %param.33, bf16[256,2048]{0,1:T(8,128)(2,1)S(1)} %bitcast.284), kind=kOutput, calls=%fused_computation.92 | convolution fusion | flops 537394688 | bytes 5769216 | tf_op jit(solution)/shard_map/dot_general | solution.py:134
  35.8 6.9 %all-to-all-start.1 = ((f32[16,1,32,256]{3,2,1,0:T(8,128)}), f32[16,1,32,256]{3,2,1,0:T(8,128)S(1)}, u32[]{:S(2)}, u32[]{:S(2)}) async-start(f32[16,1,32,256]{3,2,1,0:T(8,128)} %bitcast.32), calls=%async_computation.1 | async-start | bytes 1048576 | tf_op jit(solution)/shard_map/all_to_all | solution.py:83
  42.7 2.0 copy.163
  47.1 1.3 copy.165
  48.4 4.0 %all-to-all-done.1 = f32[16,1,32,256]{3,2,1,0:T(8,128)S(1)} async-done(((f32[16,1,32,256]{3,2,1,0:T(8,128)}), f32[16,1,32,256]{3,2,1,0:T(8,128)S(1)}, u32[]{:S(2)}, u32[]{:S(2)}) %all-to-all-start.1) | async-done | bytes 524320 | tf_op jit(solution)/shard_map/all_to_all | solution.py:83
  52.4 5.5 %all-to-all-start = ((f32[16,3,32,256]{3,2,1,0:T(8,128)}), f32[16,3,32,256]{3,2,1,0:T(8,128)}, u32[]{:S(2)}, u32[]{:S(2)}) async-start(f32[16,3,32,256]{3,2,1,0:T(8,128)} %copy.165), calls=%async_computation | async-start | bytes 3145728 | tf_op jit(solution)/shard_map/all_to_all | solution.py:83
  58.6 1.7 multiply_subtract_fusion.3
  61.0 1.4 fusion.40
  62.4 1.4 convolution_add_fusion.8
  63.8 15.1 %all-to-all-done = f32[16,3,32,256]{3,2,1,0:T(8,128)} async-done(((f32[16,3,32,256]{3,2,1,0:T(8,128)}), f32[16,3,32,256]{3,2,1,0:T(8,128)}, u32[]{:S(2)}, u32[]{:S(2)}) %all-to-all-start) | async-done | bytes 1572896 | tf_op jit(solution)/shard_map/all_to_all | solution.py:83
  78.9 2.3 copy.166
  83.2 1.6 fusion.5
  84.8 1.6 fusion.1
  86.4 1.6 convolution_add_fusion
  88.0 1.8 convolution_add_fusion.1
  97.4 1.9 multiply_add_fusion.1
  100.4 1.1 convolution_add_fusion.3
  101.6 1.6 copy.189
  103.1 5.4 %all-to-all-start.2 = ((f32[16,2,32,256]{3,2,1,0:T(8,128)}), f32[16,2,32,256]{3,2,1,0:T(8,128)}, u32[]{:S(2)}, u32[]{:S(2)}) async-start(f32[16,2,32,256]{3,2,1,0:T(8,128)} %copy.189), calls=%async_computation.2 | async-start | bytes 2097152 | tf_op jit(solution)/shard_map/all_to_all | solution.py:88
  111.2 1.6 copy.200
  112.8 1.4 collective-permute-start.3
  114.2 9.9 %all-to-all-done.2 = f32[16,2,32,256]{3,2,1,0:T(8,128)} async-done(((f32[16,2,32,256]{3,2,1,0:T(8,128)}), f32[16,2,32,256]{3,2,1,0:T(8,128)}, u32[]{:S(2)}, u32[]{:S(2)}) %all-to-all-start.2) | async-done | bytes 1048608 | tf_op jit(solution)/shard_map/all_to_all | solution.py:88
  124.0 1.4 fusion.59
  126.7 1.3 fusion.44
  128.2 2.2 fusion
  130.4 2.5 maximum_multiply_fusion
  132.9 14.3 %collective-permute-done.3 = f32[16,2,32,256]{3,2,1,0:T(8,128)} collective-permute-done((f32[16,2,32,256]{3,2,1,0:T(8,128)}, f32[16,2,32,256]{3,2,1,0:T(8,128)}, u32[]{:S(2)}, u32[]{:S(2)}) %collective-permute-start.3) | collective-permute-done | bytes 1048608 | tf_op jit(solution)/shard_map/ppermute | solution.py:97
  147.2 2.9 %copy_add_fusion = f32[16,2,32,256]{3,2,1,0:T(8,128)} fusion(f32[16,2,32,256]{3,2,1,0:T(8,128)} %collective-permute-done.3, f32[16,2,32,256]{3,0,2,1:T(8,128)S(1)} %bitcast.281), kind=kLoop, calls=%fused_computation.125 | loop fusion | flops 262144 | bytes 3145728 | tf_op jit(solution)/shard_map/add | solution.py:97
  150.1 5.7 %all-to-all-start.4 = ((f32[16,2,32,256]{3,2,1,0:T(8,128)}), f32[16,2,32,256]{3,2,1,0:T(8,128)S(1)}, u32[]{:S(2)}, u32[]{:S(2)}) async-start(f32[16,2,32,256]{3,2,1,0:T(8,128)} %copy_add_fusion), calls=%async_computation.4 | async-start | bytes 2097152 | tf_op jit(solution)/shard_map/all_to_all | solution.py:88
  155.8 4.0 %copy.210 = bf16[2048,512]{1,0:T(8,128)(2,1)} copy(bf16[2048,512]{0,1:T(8,128)(2,1)} %bitcast.292) | data formatting | bytes 4194304 | tf_op jit(solution)/shard_map/dot_general | solution.py:161
  159.8 3.8 %convolution_bitcast_fusion = f32[4,256,512]{2,1,0:T(8,128)} fusion(bf16[4,512,512]{2,1,0:T(8,128)(2,1)} %bitcast.293, bf16[1,256,1,512]{1,3,2,0:T(8,128)(2,1)S(1)} %copy-done.11), kind=kOutput, calls=%fused_computation.4 | convolution fusion | flops 536870912 | bytes 4456448 | tf_op jit(solution)/shard_map/dot_general | solution.py:161
  163.6 10.6 %all-to-all-done.4 = f32[16,2,32,256]{3,2,1,0:T(8,128)S(1)} async-done(((f32[16,2,32,256]{3,2,1,0:T(8,128)}), f32[16,2,32,256]{3,2,1,0:T(8,128)S(1)}, u32[]{:S(2)}, u32[]{:S(2)}) %all-to-all-start.4) | async-done | bytes 1048608 | tf_op jit(solution)/shard_map/all_to_all | solution.py:88
  174.2 4.5 %all-to-all-start.3 = ((f32[4,256,512]{2,1,0:T(8,128)}), f32[4,256,512]{2,1,0:T(8,128)}, u32[]{:S(2)}, u32[]{:S(2)}) async-start(f32[4,256,512]{2,1,0:T(8,128)} %convolution_bitcast_fusion), calls=%async_computation.3 | async-start | bytes 4194304 | tf_op jit(solution)/shard_map/all_to_all | solution.py:105
  178.7 2.3 fusion.9
  183.2 22.5 %all-to-all-done.3 = f32[4,256,512]{2,1,0:T(8,128)} async-done(((f32[4,256,512]{2,1,0:T(8,128)}), f32[4,256,512]{2,1,0:T(8,128)}, u32[]{:S(2)}, u32[]{:S(2)}) %all-to-all-start.3) | async-done | bytes 2097184 | tf_op jit(solution)/shard_map/all_to_all | solution.py:105
  205.7 2.4 fusion.16
  208.1 53.2 %all-reduce.4.cloned.1.call-done = (f32[512,1536]{0,1:T(8,128)}, f32[513,2048]{1,0:T(8,128)}) async-done(((f32[512,1536]{0,1:T(8,128)}, f32[513,2048]{1,0:T(8,128)}), (f32[512,1536]{0,1:T(8,128)}, f32[513,2048]{1,0:T(8,128)})) %all-reduce.4.cloned.1.call-update) | async-done | bytes 7348240 | tf_op jit(solution)/shard_map/psum | solution.py:182
  261.3 1.3 slice.103
  262.6 4.7 %slice.100 = f32[512,2048]{1,0:T(8,128)} slice(f32[513,2048]{1,0:T(8,128)} %get-tuple-element.36), slice={[0:512], [0:2048]} | slice | bytes 8388608 | tf_op jit(solution)/shard_map/slice | solution.py:187
  267.3 3.5 %copy.202 = f32[512,1536]{1,0:T(8,128)} copy(f32[512,1536]{0,1:T(8,128)} %get-tuple-element.35) | data formatting | bytes 6291456
  (105 shorter events, 23.0 us)
Async XLA Ops:
  7.2 6.5 %copy-start = (bf16[1,256,512]{2,1,0:T(8,128)(2,1)S(1)}, bf16[1,256,512]{2,1,0:T(8,128)(2,1)}, u32[]{:S(2)}) copy-start(bf16[1,256,512]{2,1,0:T(8,128)(2,1)} %param.31) | copy-start | bytes 786436
  7.2 14.6 %collective-permute-start.2 = (bf16[256,512]{1,0:T(8,128)(2,1)}, bf16[256,512]{1,0:T(8,128)(2,1)}, u32[]{:S(2)}, u32[]{:S(2)}) collective-permute-start(bf16[256,512]{1,0:T(8,128)(2,1)} %bitcast.308), channel_id=1, source_target_pairs={{0,6},{2,0},{4,2},{6,4},{1,7},{3,1},{5,3},{7,5},{8,14},{10,8},{12,... | collective-permute-start | bytes 786440 | tf_op jit(solution)/shard_map/ppermute | solution.py:123
  10.3 11.5 %collective-permute-start.1 = (bf16[256,512]{1,0:T(8,128)(2,1)}, bf16[256,512]{1,0:T(8,128)(2,1)}, u32[]{:S(2)}, u32[]{:S(2)}) collective-permute-start(bf16[256,512]{1,0:T(8,128)(2,1)} %bitcast.309), channel_id=1, source_target_pairs={{0,4},{2,6},{4,0},{6,2},{1,5},{3,7},{5,1},{7,3},{8,12},{10,14},{12... | collective-permute-start | bytes 786440 | tf_op jit(solution)/shard_map/ppermute | solution.py:123
  10.9 14.6 %collective-permute-start = (bf16[256,512]{1,0:T(8,128)(2,1)}, bf16[256,512]{1,0:T(8,128)(2,1)}, u32[]{:S(2)}, u32[]{:S(2)}) collective-permute-start(bf16[256,512]{1,0:T(8,128)(2,1)} %bitcast.310), channel_id=1, source_target_pairs={{0,2},{2,4},{4,6},{6,0},{1,3},{3,5},{5,7},{7,1},{8,10},{10,12},{12... | collective-permute-start | bytes 786440 | tf_op jit(solution)/shard_map/ppermute | solution.py:123
  13.6 1.2 copy-start.4
  13.7 11.8 %copy-start.23 = (bf16[1,256,512]{2,1,0:T(8,128)(2,1)S(1)}, bf16[1,256,512]{2,1,0:T(8,128)(2,1)}, u32[]{:S(2)}) copy-start(bf16[1,256,512]{2,1,0:T(8,128)(2,1)} %param.37) | copy-start | bytes 786436
  32.1 3.7 %copy-start.2 = (bf16[256,4,512]{0,2,1:T(8,128)(2,1)}, bf16[256,4,512]{0,2,1:T(8,128)(2,1)S(1)}, u32[]{:S(2)}) copy-start(bf16[256,4,512]{0,2,1:T(8,128)(2,1)S(1)} %copy.177) | copy-start | bytes 3145732
  35.8 9.0 %copy-start.22 = (f32[256,512]{1,0:T(8,128)S(1)}, f32[256,512]{1,0:T(8,128)}, u32[]{:S(2)}) copy-start(f32[256,512]{1,0:T(8,128)} %param.35) | copy-start | bytes 1572868
  35.8 16.6 %all-to-all-start.1 = ((f32[16,1,32,256]{3,2,1,0:T(8,128)}), f32[16,1,32,256]{3,2,1,0:T(8,128)S(1)}, u32[]{:S(2)}, u32[]{:S(2)}) async-start(f32[16,1,32,256]{3,2,1,0:T(8,128)} %bitcast.32), calls=%async_computation.1 | async-start | bytes 1048576 | tf_op jit(solution)/shard_map/all_to_all | solution.py:83
  45.8 1.0 copy-start.15
  45.8 1.2 copy-start.16
  48.4 9.6 %copy-start.24 = (f32[16,16,1]{1,0,2:T(8,128)S(1)}, f32[16,16,1]{1,0,2:T(8,128)}, u32[]{:S(2)}) copy-start(f32[16,16,1]{1,0,2:T(8,128)} %constant.73) | copy-start | bytes 3076
  48.4 10.2 %copy-start.25 = (f32[16,16,1]{1,0,2:T(8,128)S(1)}, f32[16,16,1]{1,0,2:T(8,128)}, u32[]{:S(2)}) copy-start(f32[16,16,1]{1,0,2:T(8,128)} %constant.72) | copy-start | bytes 3076
  48.4 10.2 %copy-start.26 = (f32[16,256]{1,0:T(8,128)S(1)}, f32[16,256]{1,0:T(8,128)}, u32[]{:S(2)}) copy-start(f32[16,256]{1,0:T(8,128)} %constant.63.clone) | copy-start | bytes 49156
  48.4 10.2 %copy-start.27 = (f32[16,256]{1,0:T(8,128)S(1)}, f32[16,256]{1,0:T(8,128)}, u32[]{:S(2)}) copy-start(f32[16,256]{1,0:T(8,128)} %constant.62.clone) | copy-start | bytes 49156
  52.4 5.5 %copy-start.6 = (f32[16,1,32,256]{3,2,1,0:T(8,128)}, f32[16,1,32,256]{3,2,1,0:T(8,128)S(1)}, u32[]{:S(2)}) copy-start(f32[16,1,32,256]{3,2,1,0:T(8,128)S(1)} %all-to-all-done.1) | copy-start | bytes 1572868
  52.4 26.5 %all-to-all-start = ((f32[16,3,32,256]{3,2,1,0:T(8,128)}), f32[16,3,32,256]{3,2,1,0:T(8,128)}, u32[]{:S(2)}, u32[]{:S(2)}) async-start(f32[16,3,32,256]{3,2,1,0:T(8,128)} %copy.165), calls=%async_computation | async-start | bytes 3145728 | tf_op jit(solution)/shard_map/all_to_all | solution.py:83
  58.0 2.4 copy-start.1
  60.4 2.1 copy-start.9
  86.3 1.6 copy-start.8
  90.2 1.0 copy-start.13
  90.2 1.2 copy-start.14
  96.7 0.7 copy-start.28
  96.7 0.7 copy-start.29
  103.1 20.9 %all-to-all-start.2 = ((f32[16,2,32,256]{3,2,1,0:T(8,128)}), f32[16,2,32,256]{3,2,1,0:T(8,128)}, u32[]{:S(2)}, u32[]{:S(2)}) async-start(f32[16,2,32,256]{3,2,1,0:T(8,128)} %copy.189), calls=%async_computation.2 | async-start | bytes 2097152 | tf_op jit(solution)/shard_map/all_to_all | solution.py:88
  108.6 152.8 %all-reduce.4.cloned.1.call-start = ((), (), s32[]{:S(2)}) async-start(), calls=%async_computation.5 | async-start | bytes 14811136 | tf_op jit(solution)/shard_map/psum | solution.py:182
  108.9 1.2 copy-start.7
  112.8 12.6 %copy-start.30 = (f32[512]{0:T(512)S(1)}, f32[512]{0:T(512)}, u32[]{:S(2)}) copy-start(f32[512]{0:T(512)} %param.36) | copy-start | bytes 6148
  112.8 34.5 %collective-permute-start.3 = (f32[16,2,32,256]{3,2,1,0:T(8,128)}, f32[16,2,32,256]{3,2,1,0:T(8,128)}, u32[]{:S(2)}, u32[]{:S(2)}) collective-permute-start(f32[16,2,32,256]{3,2,1,0:T(8,128)} %copy.200), channel_id=1, source_target_pairs={{0,1},{1,0},{2,3},{3,2},{4,5},{5,4},{6,7},{7,6},{8,9},{9,8},{10,11... | collective-permute-start | bytes 3145736 | tf_op jit(solution)/shard_map/ppermute | solution.py:97
  124.0 1.5 copy-start.3
  125.6 0.8 copy-start.10
  125.6 1.1 copy-start.12
  128.0 2.4 copy-start.17
  128.0 2.4 copy-start.19
  128.1 2.3 copy-start.21
  150.1 24.1 %all-to-all-start.4 = ((f32[16,2,32,256]{3,2,1,0:T(8,128)}), f32[16,2,32,256]{3,2,1,0:T(8,128)S(1)}, u32[]{:S(2)}, u32[]{:S(2)}) async-start(f32[16,2,32,256]{3,2,1,0:T(8,128)} %copy_add_fusion), calls=%async_computation.4 | async-start | bytes 2097152 | tf_op jit(solution)/shard_map/all_to_all | solution.py:88
  155.8 4.0 %copy-start.11 = (bf16[1,256,1,512]{1,3,2,0:T(8,128)(2,1)S(1)}, bf16[1,256,1,512]{1,3,2,0:T(8,128)(2,1)}, u32[]{:S(2)}) copy-start(bf16[1,256,1,512]{1,3,2,0:T(8,128)(2,1)} %copy-done.10) | copy-start | bytes 786436
  163.6 15.1 %copy-start.5 = (bf16[512,1536]{0,1:T(8,128)(2,1)S(1)}, bf16[512,1536]{0,1:T(8,128)(2,1)}, u32[]{:S(2)}) copy-start(bf16[512,1536]{0,1:T(8,128)(2,1)} %copy-done.4) | copy-start | bytes 4718596
  163.6 15.1 %copy-start.18 = (bf16[1,256,512]{1,2,0:T(8,128)(2,1)S(1)}, bf16[1,256,512]{1,2,0:T(8,128)(2,1)}, u32[]{:S(2)}) copy-start(bf16[1,256,512]{1,2,0:T(8,128)(2,1)} %copy-done.17) | copy-start | bytes 786436
  163.6 15.1 %copy-start.20 = (bf16[256,512]{0,1:T(8,128)(2,1)S(1)}, bf16[256,512]{0,1:T(8,128)(2,1)}, u32[]{:S(2)}) copy-start(bf16[256,512]{0,1:T(8,128)(2,1)} %copy-done.19) | copy-start | bytes 786436
  174.2 31.5 %all-to-all-start.3 = ((f32[4,256,512]{2,1,0:T(8,128)}), f32[4,256,512]{2,1,0:T(8,128)}, u32[]{:S(2)}, u32[]{:S(2)}) async-start(f32[4,256,512]{2,1,0:T(8,128)} %convolution_bitcast_fusion), calls=%async_computation.3 | async-start | bytes 4194304 | tf_op jit(solution)/shard_map/all_to_all | solution.py:105
Sparse Core Ops, SparseCore 0:
  133.0 128.2 all-reduce.3

commit v5 on v3

--- a/solution.py
+++ b/solution.py
@@ -43,15 +43,16 @@
     cos_b, sin_b = unit_table(second)
     cos_t, sin_t = twiddle_table(first, second)
     grid = signal.reshape(first, field_count * width, second)
-    y_re = lead_apply(cos_a, grid)
-    y_im = lead_apply(-sin_a, grid)
+    y = lead_apply(jnp.concatenate([cos_a, -sin_a], axis=0), grid)
+    y_re, y_im = (y[:first], y[first:])
     cos_t = cos_t[:, None, :]
     sin_t = sin_t[:, None, :]
-    z_re = y_re * cos_t + y_im * sin_t
-    z_im = y_im * cos_t - y_re * sin_t
-    x_re = minor_apply(z_re, cos_b) + minor_apply(z_im, sin_b)
-    x_im = minor_apply(z_im, cos_b) + minor_apply(z_re, -sin_b)
-    return x_re.reshape(signal.shape), x_im.reshape(signal.shape)
+    z = jnp.concatenate([y_re * cos_t + y_im * sin_t, y_im * cos_t - y_re * sin_t], axis=2)
+    table = jnp.concatenate(
+        [jnp.concatenate([cos_b, -sin_b], axis=1), jnp.concatenate([sin_b, cos_b], axis=1)], axis=0
+    )
+    x = minor_apply(z, table)
+    return x[..., :second].reshape(signal.shape), x[..., second:].reshape(signal.shape)
 
 
 def real_inverse(spec_re, spec_im):
@@ -60,15 +61,22 @@
     cos_a, sin_a = unit_table(first)
     cos_b, sin_b = unit_table(second)
     cos_t, sin_t = twiddle_table(first, second)
-    flat_re = spec_re.reshape(first, field_count * width, second)
-    flat_im = spec_im.reshape(first, field_count * width, second)
-    a_re = minor_apply(flat_re, cos_b) + minor_apply(flat_im, -sin_b)
-    a_im = minor_apply(flat_im, cos_b) + minor_apply(flat_re, sin_b)
+    flat = jnp.concatenate(
+        [
+            spec_re.reshape(first, field_count * width, second),
+            spec_im.reshape(first, field_count * width, second),
+        ],
+        axis=2,
+    )
+    table = jnp.concatenate(
+        [jnp.concatenate([cos_b, sin_b], axis=1), jnp.concatenate([-sin_b, cos_b], axis=1)], axis=0
+    )
+    a = minor_apply(flat, table)
+    a_re, a_im = (a[..., :second], a[..., second:])
     cos_t = cos_t[:, None, :] * (1.0 / length)
     sin_t = sin_t[:, None, :] * (1.0 / length)
-    b_re = a_re * cos_t - a_im * sin_t
-    b_im = a_re * sin_t + a_im * cos_t
-    out = lead_apply(cos_a, b_re) + lead_apply(-sin_a, b_im)
+    b = jnp.concatenate([a_re * cos_t - a_im * sin_t, a_re * sin_t + a_im * cos_t], axis=0)
+    out = lead_apply(jnp.concatenate([cos_a, -sin_a], axis=1), b)
     return out.reshape(spec_re.shape)
 
 

time: 266 us -> 265 us (level)
  matrix products: 37 us -> 29 us
  other arithmetic: 10.9 us -> 15.2 us
    dot_general x12 -> x3, matrix products: 14.6 us -> 9.11 us  [minor_apply(): return jnp.einsum('krm,mj->krj', fields, table, precision=TABLE_PRECISION)]
    dot_general x6 -> x3, matrix products: 7.99 us -> 5.34 us  [lead_apply(): return jnp.einsum('kn,nrm->krm', table, fields, precision=TABLE_PRECISION)]
    unnamed x62 -> x60, local copies, waits for them, and re-layouts: 10.9 us -> 12.8 us
where the time goes in v5:
time: 265 us; the launch traced here: 264 us
  waiting for transfers between devices  119 us (45%)
  blocking collectives  33.1 us (12%)
  local copies, waits for them, and re-layouts  31.8 us (12%)
  matrix products  29 us (11%)
  starting transfers between devices  21.5 us (8%)
  other arithmetic  15.2 us (6%)
  between operations  14.5 us (5%)
    psum x1, waiting for transfers between devices, on_device(): grad_win, joined = lax.psum((grad_win, joined), ('seq', 'rep'))  53.6 us
    all_to_all x1, blocking collectives, to_channels(): return lax.all_to_all(parts, 'seq', split_axis=0, concat_axis=0, tiled=True)  33.1 us
    all_to_all x1, waiting for transfers between devices, chan_reduce_scatter(): lax.all_to_all(pieces, 'chan', split_axis=0, concat_axis=0, tiled=True)  22.4 us
    all_to_all x2, waiting for transfers between devices, to_rows(): lax.all_to_all(fields, 'seq', split_axis=0, concat_axis=0, tiled=True)  19.8 us
    ppermute x1, waiting for transfers between devices, rep_sum(): total = total + lax.ppermute(value, 'rep', pairs)  15.4 us
    unnamed x60, local copies, waits for them, and re-layouts  12.8 us
    all_to_all x2, starting transfers between devices, to_rows(): lax.all_to_all(fields, 'seq', split_axis=0, concat_axis=0, tiled=True)  11 us
    dot_general x3, matrix products, minor_apply(): return jnp.einsum('krm,mj->krj', fields, table, precision=TABLE_PRECISION)  9.11 us
  transfers between devices with their start and end apart: 6, of which 6 were waited for; matrix products, arithmetic and copies ran while one was open for 14% of the time, Pallas kernels for 0%

profile of v5, /device:TPU:6, one launch (start us, length us, event | category | flops | bytes accessed | tf_op | source)
XLA Modules:
  0.0 263.9 jit_solution(10049143440065944096)
XLA Ops:
  7.2 1.2 copy.81
  8.4 1.0 broadcast_in_dim.7
  9.4 4.6 %all-to-all-start = ((bf16[4,256,512]{1,2,0:T(8,128)(2,1)}), bf16[4,256,512]{1,2,0:T(8,128)(2,1)S(1)}, u32[]{:S(2)}, u32[]{:S(2)}) async-start(bf16[4,256,512]{1,2,0:T(8,128)(2,1)} %broadcast_in_dim.7), calls=%async_computation | async-start | bytes 2097152 | tf_op jit(solution)/shard_map/all_to_all | solution.py:129
  14.0 1.0 copy.79
  15.0 2.0 copy.80
  17.0 1.6 copy.75
  18.6 2.0 fusion.30
  20.6 0.9 bitcast_multiply_fusion.4
  21.5 7.6 %all-to-all-done = bf16[4,256,512]{1,2,0:T(8,128)(2,1)S(1)} async-done(((bf16[4,256,512]{1,2,0:T(8,128)(2,1)}), bf16[4,256,512]{1,2,0:T(8,128)(2,1)S(1)}, u32[]{:S(2)}, u32[]{:S(2)}) %all-to-all-start) | async-done | bytes 1048608 | tf_op jit(solution)/shard_map/all_to_all | solution.py:129
  29.1 3.5 %multiply_reduce_fusion = (f32[512]{0:T(512)S(1)}, f32[256,512]{0,1:T(8,128)S(1)}, f32[256,512]{0,1:T(8,128)}) fusion(f32[3,256,1,512]{1,3,0,2:T(8,128)S(1)} %bitcast.135, f32[3,256,1,512]{1,3,2,0:T(8,128)S(1)} %bitcast.136, bf16[512,2048]{1,0:T(8,128)(2,1)} %param.27, bf16[256,2048]{0,1:T(8,128)(2,1)S(1)} %bitcast.146), kind=kOutput, calls=%fused_computation.57 | convolution fusion | flops 537394688 | bytes 5769216 | tf_op jit(solution)/shard_map/dot_general | solution.py:137
  33.1 33.1 %all_to_all.25 = f32[16,4,32,256]{3,2,1,0:T(8,128)S(1)} all-to-all(f32[16,4,32,256]{3,2,1,0:T(8,128)S(1)} %copy.83), channel_id=1, replica_groups=mesh['seq'=16,'chan'=4,'rep'=2] {'seq'}, dimensions={0} | all-to-all | bytes 4194304 | tf_op jit(solution)/shard_map/all_to_all | solution.py:91
  66.2 1.2 copy.84
  67.5 1.9 fusion.39
  70.6 0.7 copy-done.13
  71.3 5.2 %fusion = f32[16,128,512]{2,1,0:T(8,128)S(1)} fusion(f32[512,512,1]{1,0,2:T(8,128)S(1)} %copy-done.13, f32[16,128,512]{2,0,1:T(8,128)S(1)} %pad_maximum_fusion), kind=kOutput, calls=%fused_computation.2 | convolution fusion | flops 3221225472 | bytes 9437184 | tf_op jit(solution)/shard_map/krm,mj->krj/dot_general | solution.py:37
  77.1 0.6 fusion.35
  78.5 0.9 copy-done.6
  79.4 2.1 fusion.3
  81.5 1.8 fusion.7
  83.4 1.6 multiply_subtract_fusion.1
  85.7 1.7 fusion.13
  87.5 1.6 copy.87
  89.0 5.3 %all-to-all-start.2 = ((f32[16,2,32,256]{3,2,1,0:T(8,128)}), f32[16,2,32,256]{3,2,1,0:T(8,128)}, u32[]{:S(2)}, u32[]{:S(2)}) async-start(f32[16,2,32,256]{3,2,1,0:T(8,128)} %copy.87), calls=%async_computation.2 | async-start | bytes 2097152 | tf_op jit(solution)/shard_map/all_to_all | solution.py:96
  94.4 1.5 pad_maximum_fusion.2
  95.9 1.7 fusion.15
  97.6 1.6 copy.95
  99.2 1.4 collective-permute-start
  100.6 9.2 %all-to-all-done.2 = f32[16,2,32,256]{3,2,1,0:T(8,128)} async-done(((f32[16,2,32,256]{3,2,1,0:T(8,128)}), f32[16,2,32,256]{3,2,1,0:T(8,128)}, u32[]{:S(2)}, u32[]{:S(2)}) %all-to-all-start.2) | async-done | bytes 1048608 | tf_op jit(solution)/shard_map/all_to_all | solution.py:96
  109.8 1.4 fusion.38
  111.5 0.7 fusion.28
  113.1 2.2 fusion.2
  115.3 2.5 maximum_multiply_fusion
  117.8 15.4 %collective-permute-done = f32[16,2,32,256]{3,2,1,0:T(8,128)} collective-permute-done((f32[16,2,32,256]{3,2,1,0:T(8,128)}, f32[16,2,32,256]{3,2,1,0:T(8,128)}, u32[]{:S(2)}, u32[]{:S(2)}) %collective-permute-start) | collective-permute-done | bytes 1048608 | tf_op jit(solution)/shard_map/ppermute | solution.py:105
  133.2 2.9 %copy_add_fusion = f32[16,2,32,256]{3,2,1,0:T(8,128)} fusion(f32[16,2,32,256]{3,2,1,0:T(8,128)} %collective-permute-done, f32[16,2,32,256]{3,0,2,1:T(8,128)S(1)} %bitcast.145), kind=kLoop, calls=%fused_computation.73 | loop fusion | flops 262144 | bytes 3145728 | tf_op jit(solution)/shard_map/add | solution.py:105
  136.1 5.7 %all-to-all-start.4 = ((f32[16,2,32,256]{3,2,1,0:T(8,128)}), f32[16,2,32,256]{3,2,1,0:T(8,128)S(1)}, u32[]{:S(2)}, u32[]{:S(2)}) async-start(f32[16,2,32,256]{3,2,1,0:T(8,128)} %copy_add_fusion), calls=%async_computation.4 | async-start | bytes 2097152 | tf_op jit(solution)/shard_map/all_to_all | solution.py:96
  141.8 4.0 %copy.105 = bf16[2048,512]{1,0:T(8,128)(2,1)} copy(bf16[2048,512]{0,1:T(8,128)(2,1)} %bitcast.148) | data formatting | bytes 4194304 | tf_op jit(solution)/shard_map/dot_general | solution.py:164
  145.8 3.7 %convolution_bitcast_fusion = f32[4,256,512]{2,1,0:T(8,128)} fusion(bf16[4,512,512]{2,1,0:T(8,128)(2,1)} %bitcast.150, bf16[1,256,1,512]{1,3,2,0:T(8,128)(2,1)S(1)} %copy-done.8), kind=kOutput, calls=%fused_computation.23 | convolution fusion | flops 536870912 | bytes 4456448 | tf_op jit(solution)/shard_map/dot_general | solution.py:164
  149.5 10.6 %all-to-all-done.4 = f32[16,2,32,256]{3,2,1,0:T(8,128)S(1)} async-done(((f32[16,2,32,256]{3,2,1,0:T(8,128)}), f32[16,2,32,256]{3,2,1,0:T(8,128)S(1)}, u32[]{:S(2)}, u32[]{:S(2)}) %all-to-all-start.4) | async-done | bytes 1048608 | tf_op jit(solution)/shard_map/all_to_all | solution.py:96
  160.1 4.5 %all-to-all-start.3 = ((f32[4,256,512]{2,1,0:T(8,128)}), f32[4,256,512]{2,1,0:T(8,128)}, u32[]{:S(2)}, u32[]{:S(2)}) async-start(f32[4,256,512]{2,1,0:T(8,128)} %convolution_bitcast_fusion), calls=%async_computation.3 | async-start | bytes 4194304 | tf_op jit(solution)/shard_map/all_to_all | solution.py:113
  164.7 2.3 fusion.19
  167.1 1.0 copy.99
  168.1 1.0 copy.98
  169.1 22.4 %all-to-all-done.3 = f32[4,256,512]{2,1,0:T(8,128)} async-done(((f32[4,256,512]{2,1,0:T(8,128)}), f32[4,256,512]{2,1,0:T(8,128)}, u32[]{:S(2)}, u32[]{:S(2)}) %all-to-all-start.3) | async-done | bytes 2097184 | tf_op jit(solution)/shard_map/all_to_all | solution.py:113
  191.5 2.4 fusion.20
  193.9 53.6 %all-reduce.4.cloned.1.call-done = (f32[512,1536]{0,1:T(8,128)}, f32[513,2048]{1,0:T(8,128)}) async-done(((f32[512,1536]{0,1:T(8,128)}, f32[513,2048]{1,0:T(8,128)}), (f32[512,1536]{0,1:T(8,128)}, f32[513,2048]{1,0:T(8,128)})) %all-reduce.4.cloned.1.call-update) | async-done | bytes 7348240 | tf_op jit(solution)/shard_map/psum | solution.py:185
  247.5 1.3 slice.151
  248.8 4.7 %slice.146 = f32[512,2048]{1,0:T(8,128)} slice(f32[513,2048]{1,0:T(8,128)} %get-tuple-element.29), slice={[0:512], [0:2048]} | slice | bytes 8388608 | tf_op jit(solution)/shard_map/slice | solution.py:190
  253.5 3.5 %copy.97 = f32[512,1536]{1,0:T(8,128)} copy(f32[512,1536]{0,1:T(8,128)} %get-tuple-element.28) | data formatting | bytes 6291456
  (70 shorter events, 5.1 us)
Async XLA Ops:
  7.2 11.4 %copy-start = (bf16[1,256,512]{2,1,0:T(8,128)(2,1)S(1)}, bf16[1,256,512]{2,1,0:T(8,128)(2,1)}, u32[]{:S(2)}) copy-start(bf16[1,256,512]{2,1,0:T(8,128)(2,1)} %param.25) | copy-start | bytes 786436
  7.2 6.8 %copy-start.19 = (f32[256,512]{1,0:T(8,128)S(1)}, f32[256,512]{1,0:T(8,128)}, u32[]{:S(2)}) copy-start(f32[256,512]{1,0:T(8,128)} %param.28) | copy-start | bytes 1572868
  9.4 7.6 %copy-start.12 = (bf16[512,1536]{1,0:T(8,128)(2,1)S(1)}, bf16[512,1536]{1,0:T(8,128)(2,1)}, u32[]{:S(2)}) copy-start(bf16[512,1536]{1,0:T(8,128)(2,1)} %param.26) | copy-start | bytes 4718596
  9.4 19.7 %all-to-all-start = ((bf16[4,256,512]{1,2,0:T(8,128)(2,1)}), bf16[4,256,512]{1,2,0:T(8,128)(2,1)S(1)}, u32[]{:S(2)}, u32[]{:S(2)}) async-start(bf16[4,256,512]{1,2,0:T(8,128)(2,1)} %broadcast_in_dim.7), calls=%async_computation | async-start | bytes 2097152 | tf_op jit(solution)/shard_map/all_to_all | solution.py:129
  29.1 3.5 %copy-start.1 = (bf16[4,256,512]{1,2,0:T(8,128)(2,1)}, bf16[4,256,512]{1,2,0:T(8,128)(2,1)S(1)}, u32[]{:S(2)}) copy-start(bf16[4,256,512]{1,2,0:T(8,128)(2,1)S(1)} %all-to-all-done) | copy-start | bytes 3145732
  29.1 3.5 %copy-start.4 = (f32[1,256,1,512]{1,3,2,0:T(8,128)S(1)}, f32[1,256,1,512]{1,3,2,0:T(8,128)}, u32[]{:S(2)}) copy-start(f32[1,256,1,512]{1,3,2,0:T(8,128)} %bitcast_multiply_fusion.4) | copy-start | bytes 1572868
  29.1 3.5 %copy-start.10 = (f32[256,512]{0,1:T(8,128)S(1)}, f32[256,512]{0,1:T(8,128)}, u32[]{:S(2)}) copy-start(f32[256,512]{0,1:T(8,128)} %copy.79) | copy-start | bytes 1572868
  29.1 3.5 %copy-start.11 = (f32[256,512]{0,1:T(8,128)S(1)}, f32[256,512]{0,1:T(8,128)}, u32[]{:S(2)}) copy-start(f32[256,512]{0,1:T(8,128)} %copy.80) | copy-start | bytes 1572868
  66.2 1.2 copy-start.26
  67.5 1.9 copy-start.23
  67.5 1.9 copy-start.24
  70.0 1.2 copy-start.13
  78.2 1.2 copy-start.6
  81.5 1.9 copy-start.21
  81.5 1.9 copy-start.22
  85.0 0.7 copy-start.20
  89.0 20.8 %all-to-all-start.2 = ((f32[16,2,32,256]{3,2,1,0:T(8,128)}), f32[16,2,32,256]{3,2,1,0:T(8,128)}, u32[]{:S(2)}, u32[]{:S(2)}) async-start(f32[16,2,32,256]{3,2,1,0:T(8,128)} %copy.87), calls=%async_computation.2 | async-start | bytes 2097152 | tf_op jit(solution)/shard_map/all_to_all | solution.py:96
  94.3 153.2 %all-reduce.4.cloned.1.call-start = ((), (), s32[]{:S(2)}) async-start(), calls=%async_computation.5 | async-start | bytes 14811136 | tf_op jit(solution)/shard_map/psum | solution.py:185
  97.6 13.6 %copy-start.25 = (f32[512]{0:T(512)S(1)}, f32[512]{0:T(512)}, u32[]{:S(2)}) copy-start(f32[512]{0:T(512)} %param.30) | copy-start | bytes 6148
  99.2 34.0 %collective-permute-start = (f32[16,2,32,256]{3,2,1,0:T(8,128)}, f32[16,2,32,256]{3,2,1,0:T(8,128)}, u32[]{:S(2)}, u32[]{:S(2)}) collective-permute-start(f32[16,2,32,256]{3,2,1,0:T(8,128)} %copy.95), channel_id=1, source_target_pairs={{0,1},{1,0},{2,3},{3,2},{4,5},{5,4},{6,7},{7,6},{8,9},{9,8},{10,11... | collective-permute-start | bytes 3145736 | tf_op jit(solution)/shard_map/ppermute | solution.py:105
  109.8 1.4 copy-start.5
  109.8 1.7 copy-start.2
  111.5 0.8 copy-start.7
  111.5 1.1 copy-start.9
  112.9 2.4 copy-start.14
  113.0 2.4 copy-start.16
  113.0 2.3 copy-start.18
  136.1 24.1 %all-to-all-start.4 = ((f32[16,2,32,256]{3,2,1,0:T(8,128)}), f32[16,2,32,256]{3,2,1,0:T(8,128)S(1)}, u32[]{:S(2)}, u32[]{:S(2)}) async-start(f32[16,2,32,256]{3,2,1,0:T(8,128)} %copy_add_fusion), calls=%async_computation.4 | async-start | bytes 2097152 | tf_op jit(solution)/shard_map/all_to_all | solution.py:96
  141.8 4.0 %copy-start.8 = (bf16[1,256,1,512]{1,3,2,0:T(8,128)(2,1)S(1)}, bf16[1,256,1,512]{1,3,2,0:T(8,128)(2,1)}, u32[]{:S(2)}) copy-start(bf16[1,256,1,512]{1,3,2,0:T(8,128)(2,1)} %copy-done.7) | copy-start | bytes 786436
  149.5 15.1 %copy-start.3 = (bf16[512,1536]{0,1:T(8,128)(2,1)S(1)}, bf16[512,1536]{0,1:T(8,128)(2,1)}, u32[]{:S(2)}) copy-start(bf16[512,1536]{0,1:T(8,128)(2,1)} %copy.75) | copy-start | bytes 4718596
  149.5 15.1 %copy-start.15 = (bf16[1,256,512]{1,2,0:T(8,128)(2,1)S(1)}, bf16[1,256,512]{1,2,0:T(8,128)(2,1)}, u32[]{:S(2)}) copy-start(bf16[1,256,512]{1,2,0:T(8,128)(2,1)} %copy-done.14) | copy-start | bytes 786436
  149.5 15.1 %copy-start.17 = (bf16[256,512]{0,1:T(8,128)(2,1)S(1)}, bf16[256,512]{0,1:T(8,128)(2,1)}, u32[]{:S(2)}) copy-start(bf16[256,512]{0,1:T(8,128)(2,1)} %copy-done.16) | copy-start | bytes 786436
  160.1 31.4 %all-to-all-start.3 = ((f32[4,256,512]{2,1,0:T(8,128)}), f32[4,256,512]{2,1,0:T(8,128)}, u32[]{:S(2)}, u32[]{:S(2)}) async-start(f32[4,256,512]{2,1,0:T(8,128)} %convolution_bitcast_fusion), calls=%async_computation.3 | async-start | bytes 4194304 | tf_op jit(solution)/shard_map/all_to_all | solution.py:113
Sparse Core Ops, SparseCore 0:
  117.9 129.5 all-reduce.3
